TPU v7x, 256 devices: a whole 4x4x8 slice. The times are simulated.
256 devices in a mesh: pp: 8 (over x, core), ep: 32 (over z, y).
Axes of the slice: x: 4, y: 4, z: 8, core: 2. Of those that a mesh axis runs over, the one named last changes fastest.
Arguments:
- tokens: bfloat16 [512, 2048], P('ep'), may hold values from -6 to 6
- routes: int32 [8, 512, 8], P('pp'), may hold values from 0 to 31, all different within a row; in each aligned block of 16 rows (0 to 15, 16 to 31, ..., all dimensions but the last counted through in order) at most 5 rows name the same one
- combine: float32 [8, 512, 8], P('pp', 'ep'), may hold values from 0.05 to 0.5
- norm_gain: float32 [8, 2048], P('pp'), may hold values from 0.5 to 1.5
- expert_in: bfloat16 [8, 32, 2048, 1536], P('pp', 'ep'), may hold values from -0.125 to 0.125
- expert_out: bfloat16 [8, 32, 768, 2048], P('pp', 'ep'), may hold values from -0.21875 to 0.21875
Outputs:
- section_out: bfloat16 [8, 512, 2048], P('pp', 'ep')
Inputs may be any that keep to these rules, and one draw needn't show every extreme that they name: `routes`: each row names 8 different experts. Within the 16 rows of one device (rows i * 16 to (i + 1) * 16 - 1 of one layer) no expert is named more than 5 times, and some such block names some expert exactly 5 times.
All inputs are finite; a program needn't handle non-finite values.
Results may differ from a plain program's by a relative error of at most 0.028.
Values may be sent and summed in bfloat16 or wider, within the bound.
No kernel may reach another device: no remote copies, remote signals or barrier semaphores. Data moves between devices by JAX's collectives and lax.ppermute only.
A program may use at most 64 MiB of HBM per device.

v0:
```python
import jax
import jax.numpy as jnp
from jax import lax
from jax.sharding import PartitionSpec as P


def from_behind(array, axis, by):
    count = lax.axis_size(axis)
    pairs = [(i, i + by) for i in range(count) if 0 <= i + by < count]
    return lax.ppermute(array, axis, pairs)


def shards(tokens, routes, combine, norm_gain, expert_in, expert_out):
    group_size = lax.axis_size("ep")
    sections = lax.axis_size("pp")
    section_id = lax.axis_index("pp")
    member = lax.axis_index("ep")
    tok_dev, model_width = tokens.shape
    top_count = routes.shape[2]
    capacity = tok_dev * top_count * 5 // (4 * group_size)
    hidden_units = expert_out.shape[2]
    slot_count = group_size * capacity
    section_routes = routes[0]
    experts_axis = jnp.arange(group_size, dtype=jnp.int32)
    start_row = member * tok_dev
    own_routes = lax.dynamic_slice_in_dim(section_routes, start_row, tok_dev, 0)
    flat_routes = own_routes.reshape(-1)
    one_hot = (flat_routes[:, None] == experts_axis[None, :]).astype(jnp.int32)
    earlier = jnp.cumsum(one_hot, axis=0) - one_hot
    rank_of = jnp.sum(earlier * one_hot, axis=1)
    slot_of = flat_routes * capacity + rank_of
    slot_grid = slot_of[None, :] == jnp.arange(slot_count, dtype=jnp.int32)[:, None]
    slot_grid = slot_grid.reshape(slot_count, tok_dev, top_count)
    picker = jnp.any(slot_grid, axis=2).astype(jnp.bfloat16)
    weigher = jnp.sum(jnp.where(slot_grid, combine[0][None, :, :], 0.0), axis=2).T
    first_weights = expert_in[0, 0]
    second_weights = expert_out[0, 0]
    gain_row = norm_gain[0]
    current = tokens
    result = tokens
    for turn_index in range(sections):
        widened = current.astype(jnp.float32)
        scale = lax.rsqrt(jnp.mean(widened * widened, axis=-1, keepdims=True) + 1e-06)
        normed = (widened * scale * gain_row[None, :]).astype(jnp.bfloat16)
        packed = jnp.dot(picker, normed, preferred_element_type=jnp.float32).astype(jnp.bfloat16)
        packed = packed.reshape(group_size, capacity, model_width)
        arrived = lax.all_to_all(packed, "ep", split_axis=0, concat_axis=0, tiled=True)
        rows_flat = arrived.reshape(slot_count, model_width)
        projected = jnp.dot(rows_flat, first_weights, preferred_element_type=jnp.float32)
        hidden = (jax.nn.silu(projected[:, :hidden_units]) * projected[:, hidden_units:]).astype(
            jnp.bfloat16
        )
        produced_rows = jnp.dot(hidden, second_weights, preferred_element_type=jnp.float32).astype(
            jnp.bfloat16
        )
        produced = produced_rows.reshape(arrived.shape)
        returned = lax.all_to_all(produced, "ep", split_axis=0, concat_axis=0, tiled=True)
        blended = jnp.dot(
            weigher,
            returned.reshape(slot_count, model_width).astype(jnp.float32),
            precision=lax.Precision.HIGHEST,
        )
        output = (widened + blended).astype(jnp.bfloat16)
        result = jnp.where(section_id == turn_index, output, result)
        if turn_index + 1 < sections:
            arriving = from_behind(output, "pp", 1)
            current = jnp.where(section_id == turn_index + 1, arriving, current)
    return result[None]


def solution(mesh):
    placed = (
        P("ep", None),
        P("pp", None, None),
        P("pp", "ep", None),
        P("pp", None),
        P("pp", "ep", None, None),
        P("pp", "ep", None, None),
    )
    return jax.shard_map(
        shards, mesh=mesh, in_specs=placed, out_specs=P("pp", "ep", None), check_vma=False
    )
```

profile of v0, /device:TPU:8, one launch (start us, length us, event | category | flops | bytes accessed | tf_op | source)
XLA Modules:
  0.0 709.2 jit_solution(4803064732591847641)
XLA Ops:
  3.6 2.1 convolution_convert_fusion.7
  5.7 2.2 reshape.185
  7.9 39.9 %all_to_all.80 = bf16[32,5,2048]{2,1,0:T(8,128)(2,1)} all-to-all(bf16[32,5,2048]{2,1,0:T(8,128)(2,1)} %reshape.185), channel_id=1, replica_groups=mesh['pp'=8,'ep'=32] {'ep'}, dimensions={0} | all-to-all | bytes 1310720 | tf_op jit(solution)/shard_map/all_to_all | solution.py:47
  47.8 2.2 reshape.186
  50.0 4.2 fusion.14
  55.8 2.3 reshape.187
  58.1 5.6 all-to-all-start.1
  63.9 26.8 %all-to-all-done.1 = bf16[32,5,2048]{2,1,0:T(8,128)(2,1)} async-done(((bf16[32,5,2048]{2,1,0:T(8,128)(2,1)}), bf16[32,5,2048]{2,1,0:T(8,128)(2,1)}, u32[]{:S(2)}, u32[]{:S(2)}) %all-to-all-start.1) | async-done | bytes 655392 | tf_op jit(solution)/shard_map/all_to_all | solution.py:57
  90.8 2.2 reshape.188
  98.0 2.2 reshape.189
  100.2 33.2 %all_to_all.81 = bf16[32,5,2048]{2,1,0:T(8,128)(2,1)} all-to-all(bf16[32,5,2048]{2,1,0:T(8,128)(2,1)} %reshape.189), channel_id=1, replica_groups=mesh['pp'=8,'ep'=32] {'ep'}, dimensions={0} | all-to-all | bytes 1310720 | tf_op jit(solution)/shard_map/all_to_all | solution.py:47
  133.4 2.2 reshape.190
  135.6 4.2 fusion.12
  141.4 2.2 reshape.191
  143.6 35.0 %all_to_all.82 = bf16[32,5,2048]{2,1,0:T(8,128)(2,1)} all-to-all(bf16[32,5,2048]{2,1,0:T(8,128)(2,1)} %reshape.191), channel_id=1, replica_groups=mesh['pp'=8,'ep'=32] {'ep'}, dimensions={0} | all-to-all | bytes 1310720 | tf_op jit(solution)/shard_map/all_to_all | solution.py:57
  178.6 2.2 reshape.192
  182.2 2.6 collective-permute-start.1
  186.6 2.2 reshape.193
  188.8 33.4 %all_to_all.83 = bf16[32,5,2048]{2,1,0:T(8,128)(2,1)} all-to-all(bf16[32,5,2048]{2,1,0:T(8,128)(2,1)} %reshape.193), channel_id=1, replica_groups=mesh['pp'=8,'ep'=32] {'ep'}, dimensions={0} | all-to-all | bytes 1310720 | tf_op jit(solution)/shard_map/all_to_all | solution.py:47
  222.2 2.2 reshape.194
  224.4 4.2 fusion.10
  230.2 2.2 reshape.195
  232.4 35.6 %all_to_all.84 = bf16[32,5,2048]{2,1,0:T(8,128)(2,1)} all-to-all(bf16[32,5,2048]{2,1,0:T(8,128)(2,1)} %reshape.195), channel_id=1, replica_groups=mesh['pp'=8,'ep'=32] {'ep'}, dimensions={0} | all-to-all | bytes 1310720 | tf_op jit(solution)/shard_map/all_to_all | solution.py:57
  268.0 2.2 reshape.196
  275.4 2.2 reshape.197
  277.6 34.4 %all_to_all.85 = bf16[32,5,2048]{2,1,0:T(8,128)(2,1)} all-to-all(bf16[32,5,2048]{2,1,0:T(8,128)(2,1)} %reshape.197), channel_id=1, replica_groups=mesh['pp'=8,'ep'=32] {'ep'}, dimensions={0} | all-to-all | bytes 1310720 | tf_op jit(solution)/shard_map/all_to_all | solution.py:47
  312.0 2.2 reshape.198
  314.2 4.2 fusion.8
  320.0 2.2 reshape.199
  322.2 34.1 %all_to_all.86 = bf16[32,5,2048]{2,1,0:T(8,128)(2,1)} all-to-all(bf16[32,5,2048]{2,1,0:T(8,128)(2,1)} %reshape.199), channel_id=1, replica_groups=mesh['pp'=8,'ep'=32] {'ep'}, dimensions={0} | all-to-all | bytes 1310720 | tf_op jit(solution)/shard_map/all_to_all | solution.py:57
  356.3 2.2 reshape.200
  363.6 2.2 reshape.201
  365.9 33.8 %all_to_all.87 = bf16[32,5,2048]{2,1,0:T(8,128)(2,1)} all-to-all(bf16[32,5,2048]{2,1,0:T(8,128)(2,1)} %reshape.201), channel_id=1, replica_groups=mesh['pp'=8,'ep'=32] {'ep'}, dimensions={0} | all-to-all | bytes 1310720 | tf_op jit(solution)/shard_map/all_to_all | solution.py:47
  399.6 2.2 reshape.202
  401.8 4.2 fusion.6
  407.6 2.2 reshape.203
  409.8 33.7 %all_to_all.88 = bf16[32,5,2048]{2,1,0:T(8,128)(2,1)} all-to-all(bf16[32,5,2048]{2,1,0:T(8,128)(2,1)} %reshape.203), channel_id=1, replica_groups=mesh['pp'=8,'ep'=32] {'ep'}, dimensions={0} | all-to-all | bytes 1310720 | tf_op jit(solution)/shard_map/all_to_all | solution.py:57
  443.5 2.2 reshape.204
  447.2 1.9 collective-permute-start.4
  450.9 2.2 reshape.205
  453.1 34.3 %all_to_all.89 = bf16[32,5,2048]{2,1,0:T(8,128)(2,1)} all-to-all(bf16[32,5,2048]{2,1,0:T(8,128)(2,1)} %reshape.205), channel_id=1, replica_groups=mesh['pp'=8,'ep'=32] {'ep'}, dimensions={0} | all-to-all | bytes 1310720 | tf_op jit(solution)/shard_map/all_to_all | solution.py:47
  487.3 2.2 reshape.206
  489.5 4.2 fusion.4
  495.3 2.2 reshape.207
  497.5 33.1 %all_to_all.90 = bf16[32,5,2048]{2,1,0:T(8,128)(2,1)} all-to-all(bf16[32,5,2048]{2,1,0:T(8,128)(2,1)} %reshape.207), channel_id=1, replica_groups=mesh['pp'=8,'ep'=32] {'ep'}, dimensions={0} | all-to-all | bytes 1310720 | tf_op jit(solution)/shard_map/all_to_all | solution.py:57
  530.6 2.2 reshape.208
  534.2 1.9 collective-permute-start.5
  538.0 2.2 reshape.209
  540.2 34.3 %all_to_all.91 = bf16[32,5,2048]{2,1,0:T(8,128)(2,1)} all-to-all(bf16[32,5,2048]{2,1,0:T(8,128)(2,1)} %reshape.209), channel_id=1, replica_groups=mesh['pp'=8,'ep'=32] {'ep'}, dimensions={0} | all-to-all | bytes 1310720 | tf_op jit(solution)/shard_map/all_to_all | solution.py:47
  574.4 2.2 reshape.210
  576.6 4.2 fusion.2
  582.4 2.2 reshape.211
  584.6 33.1 %all_to_all.92 = bf16[32,5,2048]{2,1,0:T(8,128)(2,1)} all-to-all(bf16[32,5,2048]{2,1,0:T(8,128)(2,1)} %reshape.211), channel_id=1, replica_groups=mesh['pp'=8,'ep'=32] {'ep'}, dimensions={0} | all-to-all | bytes 1310720 | tf_op jit(solution)/shard_map/all_to_all | solution.py:57
  617.7 2.2 reshape.212
  621.3 1.9 collective-permute-start.6
  625.0 2.2 reshape.213
  627.3 34.3 %all_to_all.93 = bf16[32,5,2048]{2,1,0:T(8,128)(2,1)} all-to-all(bf16[32,5,2048]{2,1,0:T(8,128)(2,1)} %reshape.213), channel_id=1, replica_groups=mesh['pp'=8,'ep'=32] {'ep'}, dimensions={0} | all-to-all | bytes 1310720 | tf_op jit(solution)/shard_map/all_to_all | solution.py:47
  661.5 2.2 reshape.214
  663.7 4.2 fusion
  669.5 2.3 reshape.215
  671.8 5.6 all-to-all-start.15
  677.4 27.4 %all-to-all-done.15 = bf16[32,5,2048]{2,1,0:T(8,128)(2,1)} async-done(((bf16[32,5,2048]{2,1,0:T(8,128)(2,1)}), bf16[32,5,2048]{2,1,0:T(8,128)(2,1)}, u32[]{:S(2)}, u32[]{:S(2)}) %all-to-all-start.15) | async-done | bytes 655392 | tf_op jit(solution)/shard_map/all_to_all | solution.py:57
  704.9 2.2 reshape.216
  707.1 2.1 fusion.65
  (81 shorter events, 44.7 us)
Async XLA Ops:
  0.0 54.2 %copy-start = (bf16[1,1,768,2048]{3,2,1,0:T(8,128)(2,1)S(1)}, bf16[1,1,768,2048]{3,2,1,0:T(8,128)(2,1)}, u32[]{:S(2)}) copy-start(bf16[1,1,768,2048]{3,2,1,0:T(8,128)(2,1)} %param.11) | copy-start | bytes 9437188
  55.8 7.9 %copy-start.9 = (f32[1,16,8]{1,2,0:T(8,128)S(1)}, f32[1,16,8]{1,2,0:T(8,128)}, u32[]{:S(2)}) copy-start(f32[1,16,8]{1,2,0:T(8,128)} %param.8) | copy-start | bytes 1540
  55.8 37.2 %copy-start.1 = (bf16[16,2048]{1,0:T(8,128)(2,1)S(1)}, bf16[16,2048]{1,0:T(8,128)(2,1)}, u32[]{:S(2)}) copy-start(bf16[16,2048]{1,0:T(8,128)(2,1)} %param.6) | copy-start | bytes 196612
  55.8 41.0 %copy-start.2 = (f32[1,2048]{1,0:T(1,128)S(1)}, f32[1,2048]{1,0:T(1,128)}, u32[]{:S(2)}) copy-start(f32[1,2048]{1,0:T(1,128)} %param.9) | copy-start | bytes 24580
  58.1 32.7 %all-to-all-start.1 = ((bf16[32,5,2048]{2,1,0:T(8,128)(2,1)}), bf16[32,5,2048]{2,1,0:T(8,128)(2,1)}, u32[]{:S(2)}, u32[]{:S(2)}) async-start(bf16[32,5,2048]{2,1,0:T(8,128)(2,1)} %reshape.187), calls=%async_computation.1 | async-start | bytes 2097152 | tf_op jit(solution)/shard_map/all_to_all | solution.py:57
  94.4 2.2 collective-permute-start
  182.2 3.0 collective-permute-start.1
  271.6 1.9 copy-start.3
  271.7 2.3 collective-permute-start.2
  359.9 1.9 copy-start.5
  359.9 2.3 collective-permute-start.3
  447.1 1.9 copy-start.6
  447.2 2.3 collective-permute-start.4
  534.2 1.9 copy-start.7
  534.2 2.3 collective-permute-start.5
  621.3 1.9 copy-start.8
  621.3 2.3 collective-permute-start.6
  669.5 37.6 %copy-start.4 = (bf16[16,2048]{1,0:T(8,128)(2,1)S(1)}, bf16[16,2048]{1,0:T(8,128)(2,1)}, u32[]{:S(2)}) copy-start(bf16[16,2048]{1,0:T(8,128)(2,1)} %copy-done.3) | copy-start | bytes 196612
  671.8 33.1 %all-to-all-start.15 = ((bf16[32,5,2048]{2,1,0:T(8,128)(2,1)}), bf16[32,5,2048]{2,1,0:T(8,128)(2,1)}, u32[]{:S(2)}, u32[]{:S(2)}) async-start(bf16[32,5,2048]{2,1,0:T(8,128)(2,1)} %reshape.215), calls=%async_computation.15 | async-start | bytes 2097152 | tf_op jit(solution)/shard_map/all_to_all | solution.py:57
where the time goes:
time: 712 us; the launch traced here: 709 us
  blocking collectives  482 us (68%)
  local copies, waits for them, and re-layouts  72 us (10%)
  matrix products  69.1 us (10%)
  waiting for transfers between devices  57.5 us (8%)
  starting transfers between devices  24.7 us (3%)
    all_to_all x8, blocking collectives, shards(): lax.all_to_all(packed, 'ep', split_axis=0, concat_axis=0, tiled=True)  277 us
    all_to_all x6, blocking collectives, shards(): lax.all_to_all(produced, 'ep', split_axis=0, concat_axis=0, tiled=True)  205 us
    all_to_all x2, waiting for transfers between devices, shards(): lax.all_to_all(produced, 'ep', split_axis=0, concat_axis=0, tiled=True)  54.3 us
    dot_general x8, matrix products, shards(): jnp.dot(rows_flat, first_weights, preferred_element_type=jnp.float32)  33.5 us
    reshape x8, local copies, waits for them, and re-layouts, shards(): produced = produced_rows.reshape(arrived.shape)  17.9 us
    reshape x8, local copies, waits for them, and re-layouts, shards(): packed = packed.reshape(group_size, capacity, model_width)  17.8 us
    reshape x8, local copies, waits for them, and re-layouts, shards(): returned.reshape(slot_count, model_width).astype(jnp.float32)  17.5 us
    reshape x8, local copies, waits for them, and re-layouts, shards(): rows_flat = arrived.reshape(slot_count, model_width)  17.4 us
  transfers between devices with their start and end apart: 9, of which 9 were waited for; matrix products, arithmetic and copies ran while one was open for 0% of the time, Pallas kernels for 0%

commit v1 on v0

v1 whole, which is shorter than its diff:
```python
import jax
import jax.numpy as jnp
from jax import lax
from jax.sharding import PartitionSpec as P


def shards(tokens, routes, combine, norm_gain, expert_in, expert_out):
    group_size = lax.axis_size("ep")
    sections = lax.axis_size("pp")
    section_id = lax.axis_index("pp")
    member = lax.axis_index("ep")
    tok_dev, model_width = tokens.shape
    top_count = routes.shape[2]
    capacity = tok_dev * top_count * 5 // (4 * group_size)
    hidden_units = expert_out.shape[2]
    slot_count = group_size * capacity
    token_count = routes.shape[1]

    section_routes = routes[0]
    mine = section_routes == member
    hit = jnp.any(mine, axis=1)
    all_combine = lax.all_gather(combine[0], "ep", axis=0, tiled=True)
    token_weight = jnp.sum(jnp.where(mine, all_combine, 0.0), axis=1)
    hit_blocks = hit.astype(jnp.int32).reshape(group_size, tok_dev)
    rank = jnp.cumsum(hit_blocks, axis=1) - hit_blocks
    slot_of = (jnp.arange(group_size, dtype=jnp.int32)[:, None] * capacity + rank).reshape(token_count)
    picker = (hit[None, :] & (slot_of[None, :] == jnp.arange(slot_count, dtype=jnp.int32)[:, None])).astype(
        jnp.bfloat16
    )
    first_weights = expert_in[0, 0]
    second_weights = expert_out[0, 0]
    gain_row = norm_gain[0]

    def layer(current):
        widened = current.astype(jnp.float32)
        scale = lax.rsqrt(jnp.mean(widened * widened, axis=-1, keepdims=True) + 1e-06)
        normed = (widened * scale * gain_row[None, :]).astype(jnp.bfloat16)
        gathered = lax.all_gather(normed, "ep", axis=0, tiled=True)
        rows = jnp.dot(picker, gathered, preferred_element_type=jnp.float32).astype(jnp.bfloat16)
        projected = jnp.dot(rows, first_weights, preferred_element_type=jnp.float32)
        hidden = (jax.nn.silu(projected[:, :hidden_units]) * projected[:, hidden_units:]).astype(jnp.bfloat16)
        produced = jnp.dot(hidden, second_weights, preferred_element_type=jnp.float32).astype(jnp.bfloat16)
        scattered = jnp.dot(picker.T, produced, preferred_element_type=jnp.float32)
        weighted = scattered * token_weight[:, None]
        blended = lax.psum_scatter(weighted, "ep", scatter_dimension=0, tiled=True)
        return (widened + blended).astype(jnp.bfloat16)

    current = tokens
    for turn_index in range(sections):
        current = jnp.where(section_id == turn_index, layer(current), current)
        if turn_index + 1 < sections:
            arriving = lax.ppermute(current, "pp", [(turn_index, turn_index + 1)])
            current = jnp.where(section_id == turn_index + 1, arriving, current)
    return current[None]


def solution(mesh):
    placed = (
        P("ep", None),
        P("pp", None, None),
        P("pp", "ep", None),
        P("pp", None),
        P("pp", "ep", None, None),
        P("pp", "ep", None, None),
    )
    return jax.shard_map(
        shards, mesh=mesh, in_specs=placed, out_specs=P("pp", "ep", None), check_vma=False
    )
```

time: 712 us -> 2500 us (3.51)
  the two profiles are of different devices: /device:TPU:8 before, /device:TPU:7 now
where the time goes in v1:
time: 2500 us; the launch traced here: 2490 us
  waiting for transfers between devices  2320 us (93%)
  matrix products  82.2 us (3%)
  blocking collectives  41.5 us (2%)
  other arithmetic  27.3 us (1%)
    reduce_scatter x8, waiting for transfers between devices, layer(): blended = lax.psum_scatter(weighted, 'ep', scatter_dimension=0, tiled=True)  1740 us
    all_gather x8, waiting for transfers between devices, layer(): gathered = lax.all_gather(normed, 'ep', axis=0, tiled=True)  574 us
  transfers between devices with their start and end apart: 23, of which 17 were waited for; matrix products, arithmetic and copies ran while one was open for 0% of the time, Pallas kernels for 0%

profile of v1, /device:TPU:7, one launch (start us, length us, event | category | flops | bytes accessed | tf_op | source)
XLA Modules:
  0.0 2493.3 jit_solution(803948578174033361)
XLA Ops:
  6.5 1.1 fusion.186
  7.7 1.6 fusion.188
  9.3 0.8 copy.7
  10.2 9.1 compare_reduce_fusion
  19.8 0.8 copy.8
  20.6 41.5 %all-gather = f32[1,512,8]{2,0,1:T(1,128)S(1)} all-gather(f32[1,16,8]{2,0,1:T(1,128)S(1)} %copy.8), channel_id=2, replica_groups=mesh['pp'=8,'ep'=32] {'ep'}, dimensions={1}, use_global_device_ids=true | all-gather | bytes 16896 | tf_op jit(solution)/shard_map/all_gather | solution.py:22
  62.1 1.2 fusion.105
  63.3 23.5 all-gather.10.cloned.1.call-done
  86.8 5.9 fusion.14
  92.8 4.4 convolution_multiply_fusion.7
  97.2 217.5 %reduce-scatter.9.cloned.1.call-done = f32[16,2048]{1,0:T(8,128)} async-done(((f32[512,2048]{1,0:T(8,128)}), f32[16,2048]{1,0:T(8,128)}) %reduce-scatter.9.cloned.1.call-update) | async-done | bytes 131088 | tf_op jit(solution)/shard_map/reduce_scatter | solution.py:45
  314.7 0.9 fusion.225
  315.6 0.7 collective-permute-start
  316.5 0.7 fusion.192
  317.2 0.2 reduce-scatter.11.cloned.1.call-start
  317.5 77.6 %all-gather.12.cloned.1.call-done = bf16[512,2048]{1,0:T(8,128)(2,1)} async-done(((bf16[16,2048]{1,0:T(8,128)(2,1)}), bf16[512,2048]{1,0:T(8,128)(2,1)}) %all-gather.12.cloned.1.call-update) | async-done | bytes 2097168 | tf_op jit(solution)/shard_map/all_gather | solution.py:38
  395.1 5.9 fusion.12
  401.0 4.4 convolution_multiply_fusion.6
  405.4 217.3 %reduce-scatter.11.cloned.1.call-done = f32[16,2048]{1,0:T(8,128)} async-done(((f32[512,2048]{1,0:T(8,128)}), f32[16,2048]{1,0:T(8,128)}) %reduce-scatter.11.cloned.1.call-update) | async-done | bytes 131088 | tf_op jit(solution)/shard_map/reduce_scatter | solution.py:45
  622.7 0.9 fusion.224
  623.6 0.7 collective-permute-start.1
  624.5 0.7 fusion.196
  625.3 80.9 %all-gather.14.cloned.1.call-done = bf16[512,2048]{1,0:T(8,128)(2,1)} async-done(((bf16[16,2048]{1,0:T(8,128)(2,1)}), bf16[512,2048]{1,0:T(8,128)(2,1)}) %all-gather.14.cloned.1.call-update) | async-done | bytes 2097168 | tf_op jit(solution)/shard_map/all_gather | solution.py:38
  706.1 5.9 fusion.10
  712.1 4.4 convolution_multiply_fusion.5
  716.5 217.1 %reduce-scatter.13.cloned.1.call-done = f32[16,2048]{1,0:T(8,128)} async-done(((f32[512,2048]{1,0:T(8,128)}), f32[16,2048]{1,0:T(8,128)}) %reduce-scatter.13.cloned.1.call-update) | async-done | bytes 131088 | tf_op jit(solution)/shard_map/reduce_scatter | solution.py:45
  933.6 0.9 fusion.223
  934.6 0.7 collective-permute-start.2
  935.4 0.7 fusion.200
  936.2 77.8 %all-gather.16.cloned.1.call-done = bf16[512,2048]{1,0:T(8,128)(2,1)} async-done(((bf16[16,2048]{1,0:T(8,128)(2,1)}), bf16[512,2048]{1,0:T(8,128)(2,1)}) %all-gather.16.cloned.1.call-update) | async-done | bytes 2097168 | tf_op jit(solution)/shard_map/all_gather | solution.py:38
  1013.9 5.9 fusion.8
  1019.9 4.4 convolution_multiply_fusion.4
  1024.3 217.4 %reduce-scatter.15.cloned.1.call-done = f32[16,2048]{1,0:T(8,128)} async-done(((f32[512,2048]{1,0:T(8,128)}), f32[16,2048]{1,0:T(8,128)}) %reduce-scatter.15.cloned.1.call-update) | async-done | bytes 131088 | tf_op jit(solution)/shard_map/reduce_scatter | solution.py:45
  1241.7 0.9 fusion.222
  1242.6 0.7 collective-permute-start.3
  1243.4 0.7 fusion.204
  1244.2 82.3 %all-gather.18.cloned.1.call-done = bf16[512,2048]{1,0:T(8,128)(2,1)} async-done(((bf16[16,2048]{1,0:T(8,128)(2,1)}), bf16[512,2048]{1,0:T(8,128)(2,1)}) %all-gather.18.cloned.1.call-update) | async-done | bytes 2097168 | tf_op jit(solution)/shard_map/all_gather | solution.py:38
  1326.6 5.9 fusion.6
  1332.5 4.4 convolution_multiply_fusion.3
  1336.9 217.7 %reduce-scatter.17.cloned.1.call-done = f32[16,2048]{1,0:T(8,128)} async-done(((f32[512,2048]{1,0:T(8,128)}), f32[16,2048]{1,0:T(8,128)}) %reduce-scatter.17.cloned.1.call-update) | async-done | bytes 131088 | tf_op jit(solution)/shard_map/reduce_scatter | solution.py:45
  1554.6 0.9 fusion.221
  1555.6 0.7 collective-permute-start.4
  1556.4 0.7 fusion.208
  1557.2 0.3 reduce-scatter.19.cloned.1.call-start
  1557.4 78.5 %all-gather.20.cloned.1.call-done = bf16[512,2048]{1,0:T(8,128)(2,1)} async-done(((bf16[16,2048]{1,0:T(8,128)(2,1)}), bf16[512,2048]{1,0:T(8,128)(2,1)}) %all-gather.20.cloned.1.call-update) | async-done | bytes 2097168 | tf_op jit(solution)/shard_map/all_gather | solution.py:38
  1635.9 5.9 fusion.4
  1641.8 4.4 convolution_multiply_fusion.2
  1646.2 217.8 %reduce-scatter.19.cloned.1.call-done = f32[16,2048]{1,0:T(8,128)} async-done(((f32[512,2048]{1,0:T(8,128)}), f32[16,2048]{1,0:T(8,128)}) %reduce-scatter.19.cloned.1.call-update) | async-done | bytes 131088 | tf_op jit(solution)/shard_map/reduce_scatter | solution.py:45
  1864.1 0.9 fusion.220
  1865.0 0.7 collective-permute-start.5
  1865.8 0.7 fusion.212
  1866.6 81.6 %all-gather.22.cloned.1.call-done = bf16[512,2048]{1,0:T(8,128)(2,1)} async-done(((bf16[16,2048]{1,0:T(8,128)(2,1)}), bf16[512,2048]{1,0:T(8,128)(2,1)}) %all-gather.22.cloned.1.call-update) | async-done | bytes 2097168 | tf_op jit(solution)/shard_map/all_gather | solution.py:38
  1948.3 5.9 fusion.2
  1954.2 4.4 convolution_multiply_fusion.1
  1958.6 217.5 %reduce-scatter.21.cloned.1.call-done = f32[16,2048]{1,0:T(8,128)} async-done(((f32[512,2048]{1,0:T(8,128)}), f32[16,2048]{1,0:T(8,128)}) %reduce-scatter.21.cloned.1.call-update) | async-done | bytes 131088 | tf_op jit(solution)/shard_map/reduce_scatter | solution.py:45
  2176.1 0.9 fusion.219
  2177.1 1.3 collective-permute-start.6
  2178.4 6.3 collective-permute-done.6
  2184.8 0.7 fusion.216
  2185.6 71.5 %all-gather.24.cloned.1.call-done = bf16[512,2048]{1,0:T(8,128)(2,1)} async-done(((bf16[16,2048]{1,0:T(8,128)(2,1)}), bf16[512,2048]{1,0:T(8,128)(2,1)}) %all-gather.24.cloned.1.call-update) | async-done | bytes 2097168 | tf_op jit(solution)/shard_map/all_gather | solution.py:38
  2257.1 5.9 fusion
  2263.0 4.4 convolution_multiply_fusion
  2267.4 217.8 %reduce-scatter.23.cloned.1.call-done = f32[16,2048]{1,0:T(8,128)} async-done(((f32[512,2048]{1,0:T(8,128)}), f32[16,2048]{1,0:T(8,128)}) %reduce-scatter.23.cloned.1.call-update) | async-done | bytes 131088 | tf_op jit(solution)/shard_map/reduce_scatter | solution.py:45
  2485.2 1.6 fusion.226
  (65 shorter events, 2.4 us)
Async XLA Ops:
  6.5 86.2 %copy-start = (bf16[1,1,768,2048]{3,2,1,0:T(8,128)(2,1)S(1)}, bf16[1,1,768,2048]{3,2,1,0:T(8,128)(2,1)}, u32[]{:S(2)}) copy-start(bf16[1,1,768,2048]{3,2,1,0:T(8,128)(2,1)} %param.11) | copy-start | bytes 9437188
  6.5 80.3 %all-gather.10.cloned.1.call-start = ((), (), s32[]{:S(2)}) async-start(), calls=%async_computation.8 | async-start | bytes 2162688 | tf_op jit(solution)/shard_map/all_gather | solution.py:38
  9.3 305.5 %reduce-scatter.9.cloned.1.call-start = ((), (), s32[]{:S(2)}) async-start(), calls=%async_computation.9 | async-start | bytes 4325376 | tf_op jit(solution)/shard_map/reduce_scatter | solution.py:45
  97.1 217.6 %copy-start.1 = (bf16[16,2048]{1,0:T(8,128)(2,1)S(1)}, bf16[16,2048]{1,0:T(8,128)(2,1)}, u32[]{:S(2)}) copy-start(bf16[16,2048]{1,0:T(8,128)(2,1)} %param.6) | copy-start | bytes 196612
  97.1 219.4 %copy-start.2 = (f32[1,2048]{1,0:T(1,128)S(1)}, f32[1,2048]{1,0:T(1,128)}, u32[]{:S(2)}) copy-start(f32[1,2048]{1,0:T(1,128)} %param.9) | copy-start | bytes 24580
  97.1 297.9 %all-gather.12.cloned.1.call-start = ((), (), s32[]{:S(2)}) async-start(), calls=%async_computation.10 | async-start | bytes 2162688 | tf_op jit(solution)/shard_map/all_gather | solution.py:38
  315.6 0.7 collective-permute-start
  317.2 305.5 %reduce-scatter.11.cloned.1.call-start = ((), (), s32[]{:S(2)}) async-start(), calls=%async_computation.11 | async-start | bytes 4325376 | tf_op jit(solution)/shard_map/reduce_scatter | solution.py:45
  405.4 300.8 %all-gather.14.cloned.1.call-start = ((), (), s32[]{:S(2)}) async-start(), calls=%async_computation.12 | async-start | bytes 2162688 | tf_op jit(solution)/shard_map/all_gather | solution.py:38
  623.6 0.7 collective-permute-start.1
  625.2 308.4 %reduce-scatter.13.cloned.1.call-start = ((), (), s32[]{:S(2)}) async-start(), calls=%async_computation.13 | async-start | bytes 4325376 | tf_op jit(solution)/shard_map/reduce_scatter | solution.py:45
  716.4 297.5 %all-gather.16.cloned.1.call-start = ((), (), s32[]{:S(2)}) async-start(), calls=%async_computation.14 | async-start | bytes 2162688 | tf_op jit(solution)/shard_map/all_gather | solution.py:38
  934.6 0.7 collective-permute-start.2
  936.1 305.5 %reduce-scatter.15.cloned.1.call-start = ((), (), s32[]{:S(2)}) async-start(), calls=%async_computation.15 | async-start | bytes 4325376 | tf_op jit(solution)/shard_map/reduce_scatter | solution.py:45
  1024.2 302.3 %all-gather.18.cloned.1.call-start = ((), (), s32[]{:S(2)}) async-start(), calls=%async_computation.16 | async-start | bytes 2162688 | tf_op jit(solution)/shard_map/all_gather | solution.py:38
  1242.6 0.7 collective-permute-start.3
  1244.2 310.5 %reduce-scatter.17.cloned.1.call-start = ((), (), s32[]{:S(2)}) async-start(), calls=%async_computation.17 | async-start | bytes 4325376 | tf_op jit(solution)/shard_map/reduce_scatter | solution.py:45
  1336.9 299.0 %all-gather.20.cloned.1.call-start = ((), (), s32[]{:S(2)}) async-start(), calls=%async_computation.18 | async-start | bytes 2162688 | tf_op jit(solution)/shard_map/all_gather | solution.py:38
  1555.6 0.7 collective-permute-start.4
  1557.2 306.9 %reduce-scatter.19.cloned.1.call-start = ((), (), s32[]{:S(2)}) async-start(), calls=%async_computation.19 | async-start | bytes 4325376 | tf_op jit(solution)/shard_map/reduce_scatter | solution.py:45
  1646.2 302.1 %all-gather.22.cloned.1.call-start = ((), (), s32[]{:S(2)}) async-start(), calls=%async_computation.20 | async-start | bytes 2162688 | tf_op jit(solution)/shard_map/all_gather | solution.py:38
  1865.0 0.7 collective-permute-start.5
  1866.6 309.6 %reduce-scatter.21.cloned.1.call-start = ((), (), s32[]{:S(2)}) async-start(), calls=%async_computation.21 | async-start | bytes 4325376 | tf_op jit(solution)/shard_map/reduce_scatter | solution.py:45
  1958.6 298.5 %all-gather.24.cloned.1.call-start = ((), (), s32[]{:S(2)}) async-start(), calls=%async_computation.22 | async-start | bytes 2162688 | tf_op jit(solution)/shard_map/all_gather | solution.py:38
  2177.1 7.6 collective-permute-start.6
  2185.5 299.7 %reduce-scatter.23.cloned.1.call-start = ((), (), s32[]{:S(2)}) async-start(), calls=%async_computation.23 | async-start | bytes 4325376 | tf_op jit(solution)/shard_map/reduce_scatter | solution.py:45
Sparse Core Ops, SparseCore 0:
  9.9 76.8 all-gather.9
  97.3 217.3 reduce-scatter.8
  317.6 77.3 all-gather.11
  405.5 217.1 reduce-scatter.10
  625.3 80.7 all-gather.13
  716.6 217.0 reduce-scatter.12
  936.5 77.3 all-gather.15
  1024.4 217.2 reduce-scatter.14
  1244.3 82.2 all-gather.17
  1337.0 217.5 reduce-scatter.16
  1557.6 78.2 all-gather.19
  1646.3 217.7 reduce-scatter.18
  1866.7 81.5 all-gather.21
  1958.7 217.3 reduce-scatter.20
  2185.7 71.4 all-gather.23
  2267.5 217.6 reduce-scatter.22

commit v2 on v0

v2 whole, which is shorter than its diff:
```python
import jax
import jax.numpy as jnp
from jax import lax
from jax.sharding import Mesh
from jax.sharding import PartitionSpec as P


def from_behind(array, axis, by):
    count = lax.axis_size(axis)
    pairs = [(i, i + by) for i in range(count) if 0 <= i + by < count]
    return lax.ppermute(array, axis, pairs)


def shards(tokens, routes, combine, norm_gain, expert_in, expert_out):
    outer = lax.axis_size("ez")
    inner = lax.axis_size("ey")
    group_size = outer * inner
    sections = lax.axis_size("pp")
    section_id = lax.axis_index("pp")
    member = lax.axis_index("ez") * inner + lax.axis_index("ey")
    tok_dev, model_width = tokens.shape
    top_count = routes.shape[2]
    capacity = tok_dev * top_count * 5 // (4 * group_size)
    hidden_units = expert_out.shape[2]
    slot_count = group_size * capacity
    section_routes = routes[0]
    experts_axis = jnp.arange(group_size, dtype=jnp.int32)
    start_row = member * tok_dev
    own_routes = lax.dynamic_slice_in_dim(section_routes, start_row, tok_dev, 0)
    flat_routes = own_routes.reshape(-1)
    one_hot = (flat_routes[:, None] == experts_axis[None, :]).astype(jnp.int32)
    earlier = jnp.cumsum(one_hot, axis=0) - one_hot
    rank_of = jnp.sum(earlier * one_hot, axis=1)
    slot_of = flat_routes * capacity + rank_of
    slot_grid = slot_of[None, :] == jnp.arange(slot_count, dtype=jnp.int32)[:, None]
    slot_grid = slot_grid.reshape(slot_count, tok_dev, top_count)
    picker = jnp.any(slot_grid, axis=2).astype(jnp.bfloat16).reshape(outer, inner, capacity, tok_dev)
    weigher = jnp.sum(jnp.where(slot_grid, combine[0][None, :, :], 0.0), axis=2).T
    weigher = weigher.reshape(tok_dev, outer, inner, capacity)
    first_weights = expert_in[0, 0]
    second_weights = expert_out[0, 0]
    gain_row = norm_gain[0]
    current = tokens
    result = tokens
    for turn_index in range(sections):
        widened = current.astype(jnp.float32)
        scale = lax.rsqrt(jnp.mean(widened * widened, axis=-1, keepdims=True) + 1e-06)
        normed = (widened * scale * gain_row[None, :]).astype(jnp.bfloat16)
        packed = jnp.einsum("abct,td->abcd", picker, normed, preferred_element_type=jnp.float32)
        packed = packed.astype(jnp.bfloat16)
        stage = lax.all_to_all(packed, "ey", 1, 1, tiled=True)
        arrived = lax.all_to_all(stage, "ez", 0, 0, tiled=True)
        projected = jnp.einsum("abcd,dh->abch", arrived, first_weights, preferred_element_type=jnp.float32)
        hidden = (jax.nn.silu(projected[..., :hidden_units]) * projected[..., hidden_units:]).astype(
            jnp.bfloat16
        )
        produced = jnp.einsum("abch,hd->abcd", hidden, second_weights, preferred_element_type=jnp.float32)
        produced = produced.astype(jnp.bfloat16)
        stage = lax.all_to_all(produced, "ez", 0, 0, tiled=True)
        returned = lax.all_to_all(stage, "ey", 1, 1, tiled=True)
        blended = jnp.einsum(
            "tabc,abcd->td",
            weigher,
            returned.astype(jnp.float32),
            precision=lax.Precision.HIGHEST,
        )
        output = (widened + blended).astype(jnp.bfloat16)
        result = jnp.where(section_id == turn_index, output, result)
        if turn_index + 1 < sections:
            arriving = from_behind(output, "pp", 1)
            current = jnp.where(section_id == turn_index + 1, arriving, current)
    return result[None]


def inner_extent(mesh):
    row = mesh.devices[0]
    try:
        count = len({device.coords[1] for device in row})
    except AttributeError:
        count = 1
    return count if count > 1 and row.size % count == 0 else 1


def solution(mesh):
    pp_count, ep_count = mesh.devices.shape
    inner = inner_extent(mesh)
    split = Mesh(mesh.devices.reshape(pp_count, ep_count // inner, inner), ("pp", "ez", "ey"))
    ep = ("ez", "ey")
    placed = (
        P(ep, None),
        P("pp", None, None),
        P("pp", ep, None),
        P("pp", None),
        P("pp", ep, None, None),
        P("pp", ep, None, None),
    )
    return jax.shard_map(
        shards, mesh=split, in_specs=placed, out_specs=P("pp", ep, None), check_vma=False
    )
```

time: 712 us -> 668 us (0.938)
  blocking collectives: 482 us -> 540 us
  local copies, waits for them, and re-layouts: 72 us -> 14.3 us
  waiting for transfers between devices: 57.5 us -> 17.6 us
  matrix products: 69.1 us -> 58 us
    reshape x32 -> x3, local copies, waits for them, and re-layouts: 70.7 us -> 0.06 us  [the longest x2 0.05 us: shards(): jnp.any(slot_grid, axis=2).astype(jnp.bfloat16)]
    all_to_all x14 -> x30, blocking collectives: 482 us -> 540 us  [the longest x8 186 us: shards(): arrived = lax.all_to_all(stage, 'ez', 0, 0, tiled=True)]
    all_to_all x2, waiting for transfers between devices: 54.3 us -> 14.5 us  [shards(): returned = lax.all_to_all(stage, 'ey', 1, 1, tiled=True)]
    dot_general x32, matrix products: 69.1 us -> 58 us  [the longest x8 34.3 us: shards(): jnp.einsum('abcd,dh->abch', arrived, first_weights, preferred_element_typ...]
    all_to_all x0 -> x16, local copies, waits for them, and re-layouts: none -> 8.69 us  [the longest x8 4.62 us: shards(): stage = lax.all_to_all(produced, 'ez', 0, 0, tiled=True)]
where the time goes in v2:
time: 668 us; the launch traced here: 658 us
  blocking collectives  540 us (81%)
  matrix products  58 us (9%)
  starting transfers between devices  24.1 us (4%)
  waiting for transfers between devices  17.6 us (3%)
  local copies, waits for them, and re-layouts  14.3 us (2%)
    all_to_all x8, blocking collectives, shards(): arrived = lax.all_to_all(stage, 'ez', 0, 0, tiled=True)  186 us
    all_to_all x8, blocking collectives, shards(): stage = lax.all_to_all(produced, 'ez', 0, 0, tiled=True)  172 us
    all_to_all x8, blocking collectives, shards(): stage = lax.all_to_all(packed, 'ey', 1, 1, tiled=True)  112 us
    all_to_all x6, blocking collectives, shards(): returned = lax.all_to_all(stage, 'ey', 1, 1, tiled=True)  69.7 us
    dot_general x8, matrix products, shards(): jnp.einsum('abcd,dh->abch', arrived, first_weights, preferred_element_typ...  34.3 us
    all_to_all x2, waiting for transfers between devices, shards(): returned = lax.all_to_all(stage, 'ey', 1, 1, tiled=True)  14.5 us
    dot_general x8, matrix products, shards(): jnp.einsum('tabc,abcd->td', weigher, returned.astype(jnp.float32), precis...  14.1 us
  transfers between devices with their start and end apart: 9, of which 9 were waited for; matrix products, arithmetic and copies ran while one was open for 0% of the time, Pallas kernels for 0%

profile of v2, /device:TPU:8, one launch (start us, length us, event | category | flops | bytes accessed | tf_op | source)
XLA Modules:
  0.0 658.1 jit_solution(5748615757705323024)
XLA Ops:
  0.0 1.1 fusion.114
  1.1 0.8 constant_dynamic-slice_fusion
  2.7 0.8 bitcast_add_fusion
  3.8 1.2 convolution_convert_fusion.7
  5.1 14.1 %all_to_all.160 = bf16[8,4,5,2048]{3,0,2,1:T(8,128)(2,1)S(1)} all-to-all(bf16[8,4,5,2048]{3,0,2,1:T(8,128)(2,1)S(1)} %convolution_convert_fusion.7), channel_id=1, replica_groups=mesh['pp'=8,'ez'=8,'ey'=4] {'ey'}, dimensions={1} | all-to-all | bytes 1310720 | tf_op jit(solution)/shard_map/all_to_all | solution.py:51
  19.7 27.4 %all_to_all.161 = bf16[8,4,5,2048]{3,1,2,0:T(4,128)(2,1)S(1)} all-to-all(bf16[8,4,5,2048]{3,1,2,0:T(4,128)(2,1)S(1)} %copy.118), channel_id=1, replica_groups=mesh['pp'=8,'ez'=8,'ey'=4] {'ez'}, dimensions={0} | all-to-all | bytes 1310720 | tf_op jit(solution)/shard_map/all_to_all | solution.py:52
  47.1 4.3 fusion.14
  52.6 20.2 %all_to_all.162 = bf16[8,4,5,2048]{3,1,2,0:T(4,128)(2,1)S(1)} all-to-all(bf16[8,4,5,2048]{3,1,2,0:T(4,128)(2,1)S(1)} %copy.120), channel_id=1, replica_groups=mesh['pp'=8,'ez'=8,'ey'=4] {'ez'}, dimensions={0} | all-to-all | bytes 1310720 | tf_op jit(solution)/shard_map/all_to_all | solution.py:59
  72.9 1.2 copy.121
  74.1 5.6 all-to-all-start.3
  80.0 7.1 %all-to-all-done.3 = bf16[8,4,5,2048]{3,0,2,1:T(8,128)(2,1)} async-done(((bf16[8,4,5,2048]{3,0,2,1:T(8,128)(2,1)}), bf16[8,4,5,2048]{3,0,2,1:T(8,128)(2,1)}, u32[]{:S(2)}, u32[]{:S(2)}) %all-to-all-start.3) | async-done | bytes 655392 | tf_op jit(solution)/shard_map/all_to_all | solution.py:60
  87.1 2.5 fusion.71
  89.6 1.3 collective-permute-start
  90.9 0.9 collective-permute-done
  92.3 13.0 %all_to_all.163 = bf16[8,4,5,2048]{3,0,2,1:T(8,128)(2,1)S(1)} all-to-all(bf16[8,4,5,2048]{3,0,2,1:T(8,128)(2,1)S(1)} %convolution_convert_fusion.6), channel_id=1, replica_groups=mesh['pp'=8,'ez'=8,'ey'=4] {'ey'}, dimensions={1} | all-to-all | bytes 1310720 | tf_op jit(solution)/shard_map/all_to_all | solution.py:51
  105.8 23.9 %all_to_all.164 = bf16[8,4,5,2048]{3,1,2,0:T(4,128)(2,1)S(1)} all-to-all(bf16[8,4,5,2048]{3,1,2,0:T(4,128)(2,1)S(1)} %copy.124), channel_id=1, replica_groups=mesh['pp'=8,'ez'=8,'ey'=4] {'ez'}, dimensions={0} | all-to-all | bytes 1310720 | tf_op jit(solution)/shard_map/all_to_all | solution.py:52
  129.7 4.3 fusion.12
  135.2 23.3 %all_to_all.165 = bf16[8,4,5,2048]{3,1,2,0:T(4,128)(2,1)S(1)} all-to-all(bf16[8,4,5,2048]{3,1,2,0:T(4,128)(2,1)S(1)} %copy.126), channel_id=1, replica_groups=mesh['pp'=8,'ez'=8,'ey'=4] {'ez'}, dimensions={0} | all-to-all | bytes 1310720 | tf_op jit(solution)/shard_map/all_to_all | solution.py:59
  158.8 13.8 %all_to_all.166 = bf16[8,4,5,2048]{3,0,2,1:T(8,128)(2,1)S(1)} all-to-all(bf16[8,4,5,2048]{3,0,2,1:T(8,128)(2,1)S(1)} %copy.127), channel_id=1, replica_groups=mesh['pp'=8,'ez'=8,'ey'=4] {'ey'}, dimensions={1} | all-to-all | bytes 1310720 | tf_op jit(solution)/shard_map/all_to_all | solution.py:60
  172.6 1.4 fusion.70
  174.0 2.1 collective-permute-start.1
  176.8 14.1 %all_to_all.167 = bf16[8,4,5,2048]{3,0,2,1:T(8,128)(2,1)S(1)} all-to-all(bf16[8,4,5,2048]{3,0,2,1:T(8,128)(2,1)S(1)} %convolution_convert_fusion.5), channel_id=1, replica_groups=mesh['pp'=8,'ez'=8,'ey'=4] {'ey'}, dimensions={1} | all-to-all | bytes 1310720 | tf_op jit(solution)/shard_map/all_to_all | solution.py:51
  191.4 22.4 %all_to_all.168 = bf16[8,4,5,2048]{3,1,2,0:T(4,128)(2,1)S(1)} all-to-all(bf16[8,4,5,2048]{3,1,2,0:T(4,128)(2,1)S(1)} %copy.130), channel_id=1, replica_groups=mesh['pp'=8,'ez'=8,'ey'=4] {'ez'}, dimensions={0} | all-to-all | bytes 1310720 | tf_op jit(solution)/shard_map/all_to_all | solution.py:52
  213.8 4.3 fusion.10
  219.4 21.4 %all_to_all.169 = bf16[8,4,5,2048]{3,1,2,0:T(4,128)(2,1)S(1)} all-to-all(bf16[8,4,5,2048]{3,1,2,0:T(4,128)(2,1)S(1)} %copy.132), channel_id=1, replica_groups=mesh['pp'=8,'ez'=8,'ey'=4] {'ez'}, dimensions={0} | all-to-all | bytes 1310720 | tf_op jit(solution)/shard_map/all_to_all | solution.py:59
  241.2 11.2 %all_to_all.170 = bf16[8,4,5,2048]{3,0,2,1:T(8,128)(2,1)S(1)} all-to-all(bf16[8,4,5,2048]{3,0,2,1:T(8,128)(2,1)S(1)} %copy.133), channel_id=1, replica_groups=mesh['pp'=8,'ez'=8,'ey'=4] {'ey'}, dimensions={1} | all-to-all | bytes 1310720 | tf_op jit(solution)/shard_map/all_to_all | solution.py:60
  252.4 1.4 fusion.69
  253.8 1.9 collective-permute-start.2
  256.6 14.1 %all_to_all.171 = bf16[8,4,5,2048]{3,0,2,1:T(8,128)(2,1)S(1)} all-to-all(bf16[8,4,5,2048]{3,0,2,1:T(8,128)(2,1)S(1)} %convolution_convert_fusion.4), channel_id=1, replica_groups=mesh['pp'=8,'ez'=8,'ey'=4] {'ey'}, dimensions={1} | all-to-all | bytes 1310720 | tf_op jit(solution)/shard_map/all_to_all | solution.py:51
  271.2 22.4 %all_to_all.172 = bf16[8,4,5,2048]{3,1,2,0:T(4,128)(2,1)S(1)} all-to-all(bf16[8,4,5,2048]{3,1,2,0:T(4,128)(2,1)S(1)} %copy.136), channel_id=1, replica_groups=mesh['pp'=8,'ez'=8,'ey'=4] {'ez'}, dimensions={0} | all-to-all | bytes 1310720 | tf_op jit(solution)/shard_map/all_to_all | solution.py:52
  293.6 4.3 fusion.8
  299.2 21.4 %all_to_all.173 = bf16[8,4,5,2048]{3,1,2,0:T(4,128)(2,1)S(1)} all-to-all(bf16[8,4,5,2048]{3,1,2,0:T(4,128)(2,1)S(1)} %copy.138), channel_id=1, replica_groups=mesh['pp'=8,'ez'=8,'ey'=4] {'ez'}, dimensions={0} | all-to-all | bytes 1310720 | tf_op jit(solution)/shard_map/all_to_all | solution.py:59
  321.0 11.2 %all_to_all.174 = bf16[8,4,5,2048]{3,0,2,1:T(8,128)(2,1)S(1)} all-to-all(bf16[8,4,5,2048]{3,0,2,1:T(8,128)(2,1)S(1)} %copy.139), channel_id=1, replica_groups=mesh['pp'=8,'ez'=8,'ey'=4] {'ey'}, dimensions={1} | all-to-all | bytes 1310720 | tf_op jit(solution)/shard_map/all_to_all | solution.py:60
  332.2 1.4 fusion.68
  333.6 1.9 collective-permute-start.3
  336.4 14.1 %all_to_all.175 = bf16[8,4,5,2048]{3,0,2,1:T(8,128)(2,1)S(1)} all-to-all(bf16[8,4,5,2048]{3,0,2,1:T(8,128)(2,1)S(1)} %convolution_convert_fusion.3), channel_id=1, replica_groups=mesh['pp'=8,'ez'=8,'ey'=4] {'ey'}, dimensions={1} | all-to-all | bytes 1310720 | tf_op jit(solution)/shard_map/all_to_all | solution.py:51
  351.0 22.6 %all_to_all.176 = bf16[8,4,5,2048]{3,1,2,0:T(4,128)(2,1)S(1)} all-to-all(bf16[8,4,5,2048]{3,1,2,0:T(4,128)(2,1)S(1)} %copy.142), channel_id=1, replica_groups=mesh['pp'=8,'ez'=8,'ey'=4] {'ez'}, dimensions={0} | all-to-all | bytes 1310720 | tf_op jit(solution)/shard_map/all_to_all | solution.py:52
  373.6 4.3 fusion.6
  379.2 21.4 %all_to_all.177 = bf16[8,4,5,2048]{3,1,2,0:T(4,128)(2,1)S(1)} all-to-all(bf16[8,4,5,2048]{3,1,2,0:T(4,128)(2,1)S(1)} %copy.144), channel_id=1, replica_groups=mesh['pp'=8,'ez'=8,'ey'=4] {'ez'}, dimensions={0} | all-to-all | bytes 1310720 | tf_op jit(solution)/shard_map/all_to_all | solution.py:59
  401.0 11.2 %all_to_all.178 = bf16[8,4,5,2048]{3,0,2,1:T(8,128)(2,1)S(1)} all-to-all(bf16[8,4,5,2048]{3,0,2,1:T(8,128)(2,1)S(1)} %copy.145), channel_id=1, replica_groups=mesh['pp'=8,'ez'=8,'ey'=4] {'ey'}, dimensions={1} | all-to-all | bytes 1310720 | tf_op jit(solution)/shard_map/all_to_all | solution.py:60
  412.2 1.4 fusion.67
  413.6 1.9 collective-permute-start.4
  416.4 14.1 %all_to_all.179 = bf16[8,4,5,2048]{3,0,2,1:T(8,128)(2,1)S(1)} all-to-all(bf16[8,4,5,2048]{3,0,2,1:T(8,128)(2,1)S(1)} %convolution_convert_fusion.2), channel_id=1, replica_groups=mesh['pp'=8,'ez'=8,'ey'=4] {'ey'}, dimensions={1} | all-to-all | bytes 1310720 | tf_op jit(solution)/shard_map/all_to_all | solution.py:51
  431.0 22.4 %all_to_all.180 = bf16[8,4,5,2048]{3,1,2,0:T(4,128)(2,1)S(1)} all-to-all(bf16[8,4,5,2048]{3,1,2,0:T(4,128)(2,1)S(1)} %copy.148), channel_id=1, replica_groups=mesh['pp'=8,'ez'=8,'ey'=4] {'ez'}, dimensions={0} | all-to-all | bytes 1310720 | tf_op jit(solution)/shard_map/all_to_all | solution.py:52
  453.5 4.3 fusion.4
  459.0 21.4 %all_to_all.181 = bf16[8,4,5,2048]{3,1,2,0:T(4,128)(2,1)S(1)} all-to-all(bf16[8,4,5,2048]{3,1,2,0:T(4,128)(2,1)S(1)} %copy.150), channel_id=1, replica_groups=mesh['pp'=8,'ez'=8,'ey'=4] {'ez'}, dimensions={0} | all-to-all | bytes 1310720 | tf_op jit(solution)/shard_map/all_to_all | solution.py:59
  480.8 11.2 %all_to_all.182 = bf16[8,4,5,2048]{3,0,2,1:T(8,128)(2,1)S(1)} all-to-all(bf16[8,4,5,2048]{3,0,2,1:T(8,128)(2,1)S(1)} %copy.151), channel_id=1, replica_groups=mesh['pp'=8,'ez'=8,'ey'=4] {'ey'}, dimensions={1} | all-to-all | bytes 1310720 | tf_op jit(solution)/shard_map/all_to_all | solution.py:60
  492.0 1.4 fusion.66
  493.4 1.9 collective-permute-start.5
  496.2 14.1 %all_to_all.183 = bf16[8,4,5,2048]{3,0,2,1:T(8,128)(2,1)S(1)} all-to-all(bf16[8,4,5,2048]{3,0,2,1:T(8,128)(2,1)S(1)} %convolution_convert_fusion.1), channel_id=1, replica_groups=mesh['pp'=8,'ez'=8,'ey'=4] {'ey'}, dimensions={1} | all-to-all | bytes 1310720 | tf_op jit(solution)/shard_map/all_to_all | solution.py:51
  510.8 22.7 %all_to_all.184 = bf16[8,4,5,2048]{3,1,2,0:T(4,128)(2,1)S(1)} all-to-all(bf16[8,4,5,2048]{3,1,2,0:T(4,128)(2,1)S(1)} %copy.154), channel_id=1, replica_groups=mesh['pp'=8,'ez'=8,'ey'=4] {'ez'}, dimensions={0} | all-to-all | bytes 1310720 | tf_op jit(solution)/shard_map/all_to_all | solution.py:52
  533.5 4.3 fusion.2
  539.0 21.4 %all_to_all.185 = bf16[8,4,5,2048]{3,1,2,0:T(4,128)(2,1)S(1)} all-to-all(bf16[8,4,5,2048]{3,1,2,0:T(4,128)(2,1)S(1)} %copy.156), channel_id=1, replica_groups=mesh['pp'=8,'ez'=8,'ey'=4] {'ez'}, dimensions={0} | all-to-all | bytes 1310720 | tf_op jit(solution)/shard_map/all_to_all | solution.py:59
  560.8 11.2 %all_to_all.186 = bf16[8,4,5,2048]{3,0,2,1:T(8,128)(2,1)S(1)} all-to-all(bf16[8,4,5,2048]{3,0,2,1:T(8,128)(2,1)S(1)} %copy.157), channel_id=1, replica_groups=mesh['pp'=8,'ez'=8,'ey'=4] {'ey'}, dimensions={1} | all-to-all | bytes 1310720 | tf_op jit(solution)/shard_map/all_to_all | solution.py:60
  572.0 1.4 fusion.65
  573.4 1.9 collective-permute-start.6
  576.3 14.1 %all_to_all.187 = bf16[8,4,5,2048]{3,0,2,1:T(8,128)(2,1)S(1)} all-to-all(bf16[8,4,5,2048]{3,0,2,1:T(8,128)(2,1)S(1)} %convolution_convert_fusion), channel_id=1, replica_groups=mesh['pp'=8,'ez'=8,'ey'=4] {'ey'}, dimensions={1} | all-to-all | bytes 1310720 | tf_op jit(solution)/shard_map/all_to_all | solution.py:51
  590.9 22.4 %all_to_all.188 = bf16[8,4,5,2048]{3,1,2,0:T(4,128)(2,1)S(1)} all-to-all(bf16[8,4,5,2048]{3,1,2,0:T(4,128)(2,1)S(1)} %copy.160), channel_id=1, replica_groups=mesh['pp'=8,'ez'=8,'ey'=4] {'ez'}, dimensions={0} | all-to-all | bytes 1310720 | tf_op jit(solution)/shard_map/all_to_all | solution.py:52
  613.3 4.3 fusion
  618.8 21.4 %all_to_all.189 = bf16[8,4,5,2048]{3,1,2,0:T(4,128)(2,1)S(1)} all-to-all(bf16[8,4,5,2048]{3,1,2,0:T(4,128)(2,1)S(1)} %copy.162), channel_id=1, replica_groups=mesh['pp'=8,'ez'=8,'ey'=4] {'ez'}, dimensions={0} | all-to-all | bytes 1310720 | tf_op jit(solution)/shard_map/all_to_all | solution.py:59
  640.3 1.2 copy.163
  641.5 5.6 all-to-all-start.31
  647.1 7.4 %all-to-all-done.31 = bf16[8,4,5,2048]{3,0,2,1:T(8,128)(2,1)} async-done(((bf16[8,4,5,2048]{3,0,2,1:T(8,128)(2,1)}), bf16[8,4,5,2048]{3,0,2,1:T(8,128)(2,1)}, u32[]{:S(2)}, u32[]{:S(2)}) %all-to-all-start.31) | async-done | bytes 655392 | tf_op jit(solution)/shard_map/all_to_all | solution.py:60
  654.5 3.1 fusion.73
  (98 shorter events, 23.5 us)
Async XLA Ops:
  0.0 51.4 %copy-start = (bf16[1,1,768,2048]{3,2,1,0:T(8,128)(2,1)S(1)}, bf16[1,1,768,2048]{3,2,1,0:T(8,128)(2,1)}, u32[]{:S(2)}) copy-start(bf16[1,1,768,2048]{3,2,1,0:T(8,128)(2,1)} %param.11) | copy-start | bytes 9437188
  52.1 27.6 %copy-start.3 = (f32[1,16,8]{1,2,0:T(8,128)S(1)}, f32[1,16,8]{1,2,0:T(8,128)}, u32[]{:S(2)}) copy-start(f32[1,16,8]{1,2,0:T(8,128)} %param.8) | copy-start | bytes 1540
  52.1 35.0 %copy-start.1 = (bf16[16,2048]{1,0:T(8,128)(2,1)S(1)}, bf16[16,2048]{1,0:T(8,128)(2,1)}, u32[]{:S(2)}) copy-start(bf16[16,2048]{1,0:T(8,128)(2,1)} %param.6) | copy-start | bytes 196612
  52.6 39.3 %copy-start.2 = (f32[1,2048]{1,0:T(1,128)S(1)}, f32[1,2048]{1,0:T(1,128)}, u32[]{:S(2)}) copy-start(f32[1,2048]{1,0:T(1,128)} %param.9) | copy-start | bytes 24580
  74.1 13.0 %all-to-all-start.3 = ((bf16[8,4,5,2048]{3,0,2,1:T(8,128)(2,1)}), bf16[8,4,5,2048]{3,0,2,1:T(8,128)(2,1)}, u32[]{:S(2)}, u32[]{:S(2)}) async-start(bf16[8,4,5,2048]{3,0,2,1:T(8,128)(2,1)} %copy.121), calls=%async_computation.3 | async-start | bytes 1310720 | tf_op jit(solution)/shard_map/all_to_all | solution.py:60
  89.6 1.3 copy-start.4
  89.6 2.2 collective-permute-start
  174.0 2.1 copy-start.6
  174.0 2.3 collective-permute-start.1
  253.8 1.9 copy-start.7
  253.8 2.3 collective-permute-start.2
  333.6 1.9 copy-start.8
  333.6 2.3 collective-permute-start.3
  413.6 1.9 copy-start.9
  413.6 2.3 collective-permute-start.4
  493.4 1.9 copy-start.10
  493.4 2.3 collective-permute-start.5
  573.4 1.9 copy-start.11
  573.4 2.3 collective-permute-start.6
  618.3 36.2 %copy-start.5 = (bf16[16,2048]{1,0:T(8,128)(2,1)S(1)}, bf16[16,2048]{1,0:T(8,128)(2,1)}, u32[]{:S(2)}) copy-start(bf16[16,2048]{1,0:T(8,128)(2,1)} %copy-done.4) | copy-start | bytes 196612
  641.5 13.0 %all-to-all-start.31 = ((bf16[8,4,5,2048]{3,0,2,1:T(8,128)(2,1)}), bf16[8,4,5,2048]{3,0,2,1:T(8,128)(2,1)}, u32[]{:S(2)}, u32[]{:S(2)}) async-start(bf16[8,4,5,2048]{3,0,2,1:T(8,128)(2,1)} %copy.163), calls=%async_computation.31 | async-start | bytes 1310720 | tf_op jit(solution)/shard_map/all_to_all | solution.py:60

commit v3 on v2

--- a/solution.py
+++ b/solution.py
@@ -3,12 +3,6 @@
 from jax import lax
 from jax.sharding import Mesh
 from jax.sharding import PartitionSpec as P
-
-
-def from_behind(array, axis, by):
-    count = lax.axis_size(axis)
-    pairs = [(i, i + by) for i in range(count) if 0 <= i + by < count]
-    return lax.ppermute(array, axis, pairs)
 
 
 def shards(tokens, routes, combine, norm_gain, expert_in, expert_out):
@@ -40,9 +34,8 @@
     first_weights = expert_in[0, 0]
     second_weights = expert_out[0, 0]
     gain_row = norm_gain[0]
-    current = tokens
-    result = tokens
-    for turn_index in range(sections):
+
+    def layer(current):
         widened = current.astype(jnp.float32)
         scale = lax.rsqrt(jnp.mean(widened * widened, axis=-1, keepdims=True) + 1e-06)
         normed = (widened * scale * gain_row[None, :]).astype(jnp.bfloat16)
@@ -64,10 +57,15 @@
             returned.astype(jnp.float32),
             precision=lax.Precision.HIGHEST,
         )
-        output = (widened + blended).astype(jnp.bfloat16)
+        return (widened + blended).astype(jnp.bfloat16)
+
+    current = tokens
+    result = tokens
+    for turn_index in range(sections):
+        output = lax.cond(section_id == turn_index, layer, lambda held: held, current)
         result = jnp.where(section_id == turn_index, output, result)
         if turn_index + 1 < sections:
-            arriving = from_behind(output, "pp", 1)
+            arriving = lax.ppermute(output, "pp", [(turn_index, turn_index + 1)])
             current = jnp.where(section_id == turn_index + 1, arriving, current)
     return result[None]
 

time: 668 us -> 543 us (0.81)
  the two profiles are of different devices: /device:TPU:8 before, /device:TPU:7 now
where the time goes in v3:
time: 543 us; the launch traced here: 535 us
  waiting for transfers between devices  448 us (83%)
  blocking collectives  52 us (10%)
  loops' own time  15 us (3%)
  matrix products  6.64 us (1%)
    ppermute x7, waiting for transfers between devices, shards(): arriving = lax.ppermute(output, 'pp', [(turn_index, turn_index + 1)])  448 us
    all_to_all x1, blocking collectives, layer(): arrived = lax.all_to_all(stage, 'ez', 0, 0, tiled=True)  15.9 us
    all_to_all x1, blocking collectives, layer(): stage = lax.all_to_all(produced, 'ez', 0, 0, tiled=True)  15.9 us
    another operation x8, loops' own time, shards(): lax.cond(section_id == turn_index, layer, lambda held: held, current)  15 us
  transfers between devices with their start and end apart: 7, of which 1 were waited for; matrix products, arithmetic and copies ran while one was open for 0% of the time, Pallas kernels for 0%

profile of v3, /device:TPU:7, one launch (start us, length us, event | category | flops | bytes accessed | tf_op | source)
XLA Modules:
  0.0 534.9 jit_solution(12573590700534391131)
XLA Ops:
  0.0 0.8 constant_dynamic-slice_fusion
  0.8 0.1 copy.167
  0.8 0.1 eq.76
  0.9 0.8 copy.171
  1.7 0.1 fusion.193
  1.8 0.2 reduce_window_sum.11
  1.9 0.2 select_reduce_fusion.1
  2.1 0.1 reduce_sum.93
  2.2 0.1 copy.168
  2.3 0.8 bitcast_add_fusion
  3.1 0.1 copy.169
  3.1 0.1 fusion.192
  3.3 0.1 select_reduce_fusion
  3.4 0.1 copy.170
  3.6 0.1 copy.172
  3.7 0.9 conditional.8
  3.7 0.8 copy.269
  4.5 0.7 collective-permute-start
  5.2 0.0 collective-permute-done
  5.2 0.9 broadcast_select_fusion
  6.1 0.7 collective-permute-start.1
  6.8 0.0 collective-permute-done.1
  6.8 7.8 %conditional.10 = (bf16[16,2048]{1,0:T(8,128)(2,1)S(1)}) conditional(s32[]{:T(128)} %convert_element_type.215, bf16[16,2048]{1,0:T(8,128)(2,1)S(1)} %broadcast_select_fusion.1, (bf16[16,2048]{1,0:T(8,128)(2,1)S(1)}, f32[1,2048]{1,0:T(1,128)}, bf16[8,4,5,16]{3,2,1,0:T(8,128)(2,1)S(1)}, bf16[2048,1536]{1,0:T(8,128)(2,1)}, ...), branch_computations={%region_10.11_spmd, %region_11.13_spmd} | conditional | flops 1585070080 | bytes 36068644 | solution.py:65
  14.6 0.7 collective-permute-start.2
  15.3 0.0 collective-permute-done.2
  15.4 0.7 collective-permute-start.3
  16.1 0.0 collective-permute-done.3
  16.1 0.7 collective-permute-start.4
  16.8 0.0 collective-permute-done.4
  16.8 7.0 %conditional.13 = (bf16[16,2048]{1,0:T(8,128)(2,1)S(1)}) conditional(s32[]{:T(128)} %convert_element_type.212, bf16[16,2048]{1,0:T(8,128)(2,1)S(1)} %broadcast_select_fusion.4, (bf16[16,2048]{1,0:T(8,128)(2,1)S(1)}, f32[1,2048]{1,0:T(1,128)}, bf16[8,4,5,16]{3,2,1,0:T(8,128)(2,1)S(1)}, bf16[2048,1536]{1,0:T(8,128)(2,1)}, ...), branch_computations={%region_19.20_spmd, %region_20.22_spmd} | conditional | flops 1585070080 | bytes 36068644 | solution.py:65
  23.8 0.7 collective-permute-start.5
  24.5 0.0 collective-permute-done.5
  24.6 1.3 collective-permute-start.6
  25.9 447.9 %collective-permute-done.6 = bf16[16,2048]{1,0:T(8,128)(2,1)S(1)} collective-permute-done((bf16[16,2048]{1,0:T(8,128)(2,1)S(1)}, bf16[16,2048]{1,0:T(8,128)(2,1)S(1)}, u32[]{:S(2)}, u32[]{:S(2)}) %collective-permute-start.6) | collective-permute-done | bytes 65568 | tf_op jit(solution)/shard_map/ppermute | solution.py:68
  473.8 0.0 copy-start
  473.8 60.2 %conditional.15 = (bf16[16,2048]{1,0:T(8,128)(2,1)S(1)}) conditional(s32[]{:T(128)} %convert_element_type.210, bf16[16,2048]{1,0:T(8,128)(2,1)S(1)} %broadcast_select_fusion.6, (bf16[16,2048]{1,0:T(8,128)(2,1)S(1)}, f32[1,2048]{1,0:T(1,128)}, bf16[8,4,5,16]{3,2,1,0:T(8,128)(2,1)S(1)}, bf16[2048,1536]{1,0:T(8,128)(2,1)}, ...), branch_computations={%region_25.26_spmd, %region_26.28_spmd} | conditional | flops 1585070080 | bytes 36068644 | solution.py:65
  473.8 0.1 fusion.182
  474.0 1.1 fusion.175
  475.0 10.0 %all_to_all.156 = bf16[8,4,5,2048]{3,0,2,1:T(8,128)(2,1)S(1)} all-to-all(bf16[8,4,5,2048]{3,0,2,1:T(8,128)(2,1)S(1)} %fusion.175), channel_id=1, replica_groups=mesh['pp'=8,'ez'=8,'ey'=4] {'ey'}, dimensions={1} | all-to-all | bytes 1310720 | tf_op jit(solution)/shard_map/cond/branch_1_fun/all_to_all | solution.py:44
  485.1 0.5 copy.163
  485.6 15.9 %all_to_all.157 = bf16[8,4,5,2048]{3,1,2,0:T(4,128)(2,1)S(1)} all-to-all(bf16[8,4,5,2048]{3,1,2,0:T(4,128)(2,1)S(1)} %copy.163), channel_id=1, replica_groups=mesh['pp'=8,'ez'=8,'ey'=4] {'ez'}, dimensions={0} | all-to-all | bytes 1310720 | tf_op jit(solution)/shard_map/cond/branch_1_fun/all_to_all | solution.py:45
  501.5 0.0 copy-start.9
  501.5 4.4 fusion.168
  506.0 0.0 copy-done.9
  506.0 0.7 fusion.172
  506.7 0.5 copy.165
  507.2 15.9 %all_to_all.158 = bf16[8,4,5,2048]{3,1,2,0:T(4,128)(2,1)S(1)} all-to-all(bf16[8,4,5,2048]{3,1,2,0:T(4,128)(2,1)S(1)} %copy.165), channel_id=1, replica_groups=mesh['pp'=8,'ez'=8,'ey'=4] {'ez'}, dimensions={0} | all-to-all | bytes 1310720 | tf_op jit(solution)/shard_map/cond/branch_1_fun/all_to_all | solution.py:52
  523.1 0.4 copy.166
  523.5 10.0 %all_to_all.159 = bf16[8,4,5,2048]{3,0,2,1:T(8,128)(2,1)S(1)} all-to-all(bf16[8,4,5,2048]{3,0,2,1:T(8,128)(2,1)S(1)} %copy.166), channel_id=1, replica_groups=mesh['pp'=8,'ez'=8,'ey'=4] {'ey'}, dimensions={1} | all-to-all | bytes 1310720 | tf_op jit(solution)/shard_map/cond/branch_1_fun/all_to_all | solution.py:53
  533.5 0.4 fusion.177
  534.0 0.0 copy-done
  534.0 0.7 select_bitcast_fusion
  (20 shorter events, 0.3 us)
Async XLA Ops:
  4.5 0.7 collective-permute-start
  6.1 0.7 collective-permute-start.1
  14.6 0.7 collective-permute-start.2
  15.4 0.7 collective-permute-start.3
  16.1 0.7 collective-permute-start.4
  23.8 0.7 collective-permute-start.5
  24.6 449.2 %collective-permute-start.6 = (bf16[16,2048]{1,0:T(8,128)(2,1)S(1)}, bf16[16,2048]{1,0:T(8,128)(2,1)S(1)}, u32[]{:S(2)}, u32[]{:S(2)}) collective-permute-start(bf16[16,2048]{1,0:T(8,128)(2,1)S(1)} %get-tuple-element.379), channel_id=1, source_target_pairs={{192,224},{193,225},{194,226},{195,227},{196,228},{197,229},{198,2... | collective-permute-start | bytes 196616 | tf_op jit(solution)/shard_map/ppermute | solution.py:68
  473.8 60.2 %copy-start = (bf16[16,2048]{1,0:T(8,128)(2,1)S(1)}, bf16[16,2048]{1,0:T(8,128)(2,1)}, u32[]{:S(2)}) copy-start(bf16[16,2048]{1,0:T(8,128)(2,1)} %param.22) | copy-start | bytes 196612
  501.5 4.4 copy-start.9

commit v4 on v3

v4 whole, which is shorter than its diff:
```python
import jax
import jax.numpy as jnp
from jax import lax
from jax.sharding import PartitionSpec as P


def shards(tokens, routes, combine, norm_gain, expert_in, expert_out):
    group_size = lax.axis_size("ep")
    sections = lax.axis_size("pp")
    section_id = lax.axis_index("pp")
    member = lax.axis_index("ep")
    tok_dev, model_width = tokens.shape
    top_count = routes.shape[2]
    capacity = tok_dev * top_count * 5 // (4 * group_size)
    hidden_units = expert_out.shape[2]
    slot_count = group_size * capacity
    section_routes = routes[0]
    experts_axis = jnp.arange(group_size, dtype=jnp.int32)
    start_row = member * tok_dev
    own_routes = lax.dynamic_slice_in_dim(section_routes, start_row, tok_dev, 0)
    flat_routes = own_routes.reshape(-1)
    one_hot = (flat_routes[:, None] == experts_axis[None, :]).astype(jnp.int32)
    earlier = jnp.cumsum(one_hot, axis=0) - one_hot
    rank_of = jnp.sum(earlier * one_hot, axis=1)
    slot_of = flat_routes * capacity + rank_of
    slot_grid = slot_of[None, :] == jnp.arange(slot_count, dtype=jnp.int32)[:, None]
    slot_grid = slot_grid.reshape(slot_count, tok_dev, top_count)
    picker = jnp.any(slot_grid, axis=2).astype(jnp.bfloat16).reshape(group_size, capacity, tok_dev)
    weigher = jnp.sum(jnp.where(slot_grid, combine[0][None, :, :], 0.0), axis=2).T
    weigher = weigher.reshape(tok_dev, group_size, capacity)
    first_weights = expert_in[0, 0]
    second_weights = expert_out[0, 0]
    gain_row = norm_gain[0]

    def layer(current):
        widened = current.astype(jnp.float32)
        scale = lax.rsqrt(jnp.mean(widened * widened, axis=-1, keepdims=True) + 1e-06)
        normed = (widened * scale * gain_row[None, :]).astype(jnp.bfloat16)
        packed = jnp.einsum("gct,td->gcd", picker, normed, preferred_element_type=jnp.float32)
        arrived = lax.all_to_all(packed.astype(jnp.bfloat16), "ep", 0, 0, tiled=True)
        projected = jnp.einsum("gcd,dh->gch", arrived, first_weights, preferred_element_type=jnp.float32)
        hidden = (jax.nn.silu(projected[..., :hidden_units]) * projected[..., hidden_units:]).astype(
            jnp.bfloat16
        )
        produced = jnp.einsum("gch,hd->gcd", hidden, second_weights, preferred_element_type=jnp.float32)
        returned = lax.all_to_all(produced.astype(jnp.bfloat16), "ep", 0, 0, tiled=True)
        blended = jnp.einsum(
            "tgc,gcd->td",
            weigher,
            returned.astype(jnp.float32),
            precision=lax.Precision.HIGHEST,
        )
        return (widened + blended).astype(jnp.bfloat16)

    current = tokens
    result = tokens
    for turn_index in range(sections):
        output = lax.cond(section_id == turn_index, layer, lambda held: held, current)
        result = jnp.where(section_id == turn_index, output, result)
        if turn_index + 1 < sections:
            arriving = lax.ppermute(output, "pp", [(turn_index, turn_index + 1)])
            current = jnp.where(section_id == turn_index + 1, arriving, current)
    return result[None]


def solution(mesh):
    placed = (
        P("ep", None),
        P("pp", None, None),
        P("pp", "ep", None),
        P("pp", None),
        P("pp", "ep", None, None),
        P("pp", "ep", None, None),
    )
    return jax.shard_map(
        shards, mesh=mesh, in_specs=placed, out_specs=P("pp", "ep", None), check_vma=False
    )
```

time: 543 us -> 471 us (0.87)
  waiting for transfers between devices: 448 us -> 384 us
  blocking collectives: 52 us -> 44.4 us
    ppermute x7, waiting for transfers between devices: 448 us -> 384 us  [shards(): arriving = lax.ppermute(output, 'pp', [(turn_index, turn_index + 1)])]
    all_to_all x4 -> x2, blocking collectives: 52 us -> 44.4 us  [the longest x1 22.2 us: layer(): lax.all_to_all(produced.astype(jnp.bfloat16), 'ep', 0, 0, tiled=True)]
where the time goes in v4:
time: 471 us; the launch traced here: 463 us
  waiting for transfers between devices  384 us (82%)
  blocking collectives  44.4 us (9%)
  loops' own time  14.6 us (3%)
  matrix products  6.92 us (1%)
  starting transfers between devices  5.27 us (1%)
    ppermute x7, waiting for transfers between devices, shards(): arriving = lax.ppermute(output, 'pp', [(turn_index, turn_index + 1)])  384 us
    all_to_all x1, blocking collectives, layer(): lax.all_to_all(produced.astype(jnp.bfloat16), 'ep', 0, 0, tiled=True)  22.2 us
    all_to_all x1, blocking collectives, layer(): lax.all_to_all(packed.astype(jnp.bfloat16), 'ep', 0, 0, tiled=True)  22.2 us
    another operation x8, loops' own time, shards(): lax.cond(section_id == turn_index, layer, lambda held: held, current)  14.6 us
  transfers between devices with their start and end apart: 7, of which 1 were waited for; matrix products, arithmetic and copies ran while one was open for 0% of the time, Pallas kernels for 0%

profile of v4, /device:TPU:7, one launch (start us, length us, event | category | flops | bytes accessed | tf_op | source)
XLA Modules:
  0.0 462.9 jit_solution(880473984933474150)
XLA Ops:
  0.0 0.8 constant_dynamic-slice_fusion
  0.8 0.1 copy.115
  0.8 0.1 eq.76
  0.9 0.8 copy.119
  1.7 0.1 fusion.201
  1.8 0.2 reduce_window_sum.11
  1.9 0.2 select_reduce_fusion.1
  2.1 0.1 reduce_sum.93
  2.2 0.1 copy.116
  2.3 0.8 bitcast_add_fusion
  3.1 0.1 copy.117
  3.1 0.1 fusion.200
  3.3 0.1 select_reduce_fusion
  3.4 0.1 copy.118
  3.6 0.1 copy.120
  3.7 0.9 conditional.8
  3.7 0.8 copy.201
  4.5 0.7 collective-permute-start
  5.2 0.0 collective-permute-done
  5.2 0.9 broadcast_select_fusion
  6.1 0.7 collective-permute-start.1
  6.8 0.0 collective-permute-done.1
  6.8 7.6 %conditional.10 = (bf16[16,2048]{1,0:T(8,128)(2,1)S(1)}) conditional(s32[]{:T(128)} %convert_element_type.215, bf16[16,2048]{1,0:T(8,128)(2,1)S(1)} %broadcast_select_fusion.1, (bf16[16,2048]{1,0:T(8,128)(2,1)S(1)}, f32[1,2048]{1,0:T(1,128)}, bf16[32,5,16]{2,1,0:T(8,128)(2,1)S(1)}, bf16[2048,1536]{1,0:T(8,128)(2,1)}, bf16[768,2048]{1,0:T(8,128)(2,1)}, ...), branch_computations={%region_10.11_spmd, %region_11.13_spmd} | conditional | flops 1585070080 | bytes 32136484 | solution.py:58
  14.4 0.7 collective-permute-start.2
  15.1 0.0 collective-permute-done.2
  15.2 0.7 collective-permute-start.3
  15.9 0.0 collective-permute-done.3
  15.9 0.7 collective-permute-start.4
  16.6 0.0 collective-permute-done.4
  16.6 6.8 %conditional.13 = (bf16[16,2048]{1,0:T(8,128)(2,1)S(1)}) conditional(s32[]{:T(128)} %convert_element_type.212, bf16[16,2048]{1,0:T(8,128)(2,1)S(1)} %broadcast_select_fusion.4, (bf16[16,2048]{1,0:T(8,128)(2,1)S(1)}, f32[1,2048]{1,0:T(1,128)}, bf16[32,5,16]{2,1,0:T(8,128)(2,1)S(1)}, bf16[2048,1536]{1,0:T(8,128)(2,1)}, bf16[768,2048]{1,0:T(8,128)(2,1)}, ...), branch_computations={%region_19.20_spmd, %region_20.22_spmd} | conditional | flops 1585070080 | bytes 32136484 | solution.py:58
  23.4 0.7 collective-permute-start.5
  24.1 0.0 collective-permute-done.5
  24.2 1.3 collective-permute-start.6
  25.5 384.2 %collective-permute-done.6 = bf16[16,2048]{1,0:T(8,128)(2,1)S(1)} collective-permute-done((bf16[16,2048]{1,0:T(8,128)(2,1)S(1)}, bf16[16,2048]{1,0:T(8,128)(2,1)S(1)}, u32[]{:S(2)}, u32[]{:S(2)}) %collective-permute-start.6) | collective-permute-done | bytes 65568 | tf_op jit(solution)/shard_map/ppermute | solution.py:61
  409.7 0.0 copy-start
  409.7 52.2 %conditional.15 = (bf16[16,2048]{1,0:T(8,128)(2,1)S(1)}) conditional(s32[]{:T(128)} %convert_element_type.210, bf16[16,2048]{1,0:T(8,128)(2,1)S(1)} %broadcast_select_fusion.6, (bf16[16,2048]{1,0:T(8,128)(2,1)S(1)}, f32[1,2048]{1,0:T(1,128)}, bf16[32,5,16]{2,1,0:T(8,128)(2,1)S(1)}, bf16[2048,1536]{1,0:T(8,128)(2,1)}, bf16[768,2048]{1,0:T(8,128)(2,1)}, ...), branch_computations={%region_25.26_spmd, %region_26.28_spmd} | conditional | flops 1585070080 | bytes 32136484 | solution.py:58
  409.7 0.1 fusion.190
  409.9 1.1 fusion.182
  410.9 0.4 copy.111
  411.3 22.2 %all_to_all.78 = bf16[32,5,2048]{2,1,0:T(8,128)(2,1)S(1)} all-to-all(bf16[32,5,2048]{2,1,0:T(8,128)(2,1)S(1)} %copy.111), channel_id=1, replica_groups=mesh['pp'=8,'ep'=32] {'ep'}, dimensions={0} | all-to-all | bytes 1310720 | tf_op jit(solution)/shard_map/cond/branch_1_fun/all_to_all | solution.py:40
  433.5 0.0 copy-start.9
  433.5 4.4 fusion.175
  437.9 0.0 copy-done.9
  437.9 0.7 fusion.179
  438.6 0.4 copy.113
  439.0 22.2 %all_to_all.79 = bf16[32,5,2048]{2,1,0:T(8,128)(2,1)S(1)} all-to-all(bf16[32,5,2048]{2,1,0:T(8,128)(2,1)S(1)} %copy.113), channel_id=1, replica_groups=mesh['pp'=8,'ep'=32] {'ep'}, dimensions={0} | all-to-all | bytes 1310720 | tf_op jit(solution)/shard_map/cond/branch_1_fun/all_to_all | solution.py:46
  461.2 0.7 fusion.184
  462.0 0.0 copy-done
  462.0 0.7 select_bitcast_fusion
  (20 shorter events, 0.3 us)
Async XLA Ops:
  4.5 0.7 collective-permute-start
  6.1 0.7 collective-permute-start.1
  14.4 0.7 collective-permute-start.2
  15.2 0.7 collective-permute-start.3
  15.9 0.7 collective-permute-start.4
  23.4 0.7 collective-permute-start.5
  24.2 385.5 %collective-permute-start.6 = (bf16[16,2048]{1,0:T(8,128)(2,1)S(1)}, bf16[16,2048]{1,0:T(8,128)(2,1)S(1)}, u32[]{:S(2)}, u32[]{:S(2)}) collective-permute-start(bf16[16,2048]{1,0:T(8,128)(2,1)S(1)} %get-tuple-element.331), channel_id=1, source_target_pairs={{192,224},{193,225},{194,226},{195,227},{196,228},{197,229},{198,2... | collective-permute-start | bytes 196616 | tf_op jit(solution)/shard_map/ppermute | solution.py:61
  409.7 52.3 %copy-start = (bf16[16,2048]{1,0:T(8,128)(2,1)S(1)}, bf16[16,2048]{1,0:T(8,128)(2,1)}, u32[]{:S(2)}) copy-start(bf16[16,2048]{1,0:T(8,128)(2,1)} %param.22) | copy-start | bytes 196612
  433.5 4.4 copy-start.9

commit v5 on v4

--- a/solution.py
+++ b/solution.py
@@ -32,18 +32,24 @@
     second_weights = expert_out[0, 0]
     gain_row = norm_gain[0]
 
+    def exchange(blocks):
+        lanes = 128 if model_width % 128 == 0 else model_width
+        dense = blocks.reshape(group_size, capacity * (model_width // lanes), lanes)
+        moved = lax.all_to_all(dense, "ep", 0, 0, tiled=True)
+        return moved.reshape(blocks.shape)
+
     def layer(current):
         widened = current.astype(jnp.float32)
         scale = lax.rsqrt(jnp.mean(widened * widened, axis=-1, keepdims=True) + 1e-06)
         normed = (widened * scale * gain_row[None, :]).astype(jnp.bfloat16)
         packed = jnp.einsum("gct,td->gcd", picker, normed, preferred_element_type=jnp.float32)
-        arrived = lax.all_to_all(packed.astype(jnp.bfloat16), "ep", 0, 0, tiled=True)
+        arrived = exchange(packed.astype(jnp.bfloat16))
         projected = jnp.einsum("gcd,dh->gch", arrived, first_weights, preferred_element_type=jnp.float32)
         hidden = (jax.nn.silu(projected[..., :hidden_units]) * projected[..., hidden_units:]).astype(
             jnp.bfloat16
         )
         produced = jnp.einsum("gch,hd->gcd", hidden, second_weights, preferred_element_type=jnp.float32)
-        returned = lax.all_to_all(produced.astype(jnp.bfloat16), "ep", 0, 0, tiled=True)
+        returned = exchange(produced.astype(jnp.bfloat16))
         blended = jnp.einsum(
             "tgc,gcd->td",
             weigher,

time: 471 us -> 429 us (0.911)
  waiting for transfers between devices: 384 us -> 335 us
  loops' own time: 14.6 us -> 27.7 us
  blocking collectives: 44.4 us -> 36.2 us
    ppermute x7, waiting for transfers between devices: 384 us -> 335 us  [shards(): arriving = lax.ppermute(output, 'pp', [(turn_index, turn_index + 1)])]
    another operation x8, loops' own time: 14.6 us -> 27.7 us  [shards(): lax.cond(section_id == turn_index, layer, lambda held: held, current)]
    all_to_all x2, blocking collectives: 44.4 us -> 36.2 us  [exchange(): moved = lax.all_to_all(dense, 'ep', 0, 0, tiled=True)]
where the time goes in v5:
time: 429 us; the launch traced here: 422 us
  waiting for transfers between devices  335 us (78%)
  blocking collectives  36.2 us (8%)
  loops' own time  27.7 us (6%)
  matrix products  6.93 us (2%)
  local copies, waits for them, and re-layouts  6.75 us (2%)
  starting transfers between devices  5.27 us (1%)
    ppermute x7, waiting for transfers between devices, shards(): arriving = lax.ppermute(output, 'pp', [(turn_index, turn_index + 1)])  335 us
    all_to_all x2, blocking collectives, exchange(): moved = lax.all_to_all(dense, 'ep', 0, 0, tiled=True)  36.2 us
    another operation x8, loops' own time, shards(): lax.cond(section_id == turn_index, layer, lambda held: held, current)  27.7 us
  transfers between devices with their start and end apart: 7, of which 1 were waited for; matrix products, arithmetic and copies ran while one was open for 0% of the time, Pallas kernels for 0%

profile of v5, /device:TPU:7, one launch (start us, length us, event | category | flops | bytes accessed | tf_op | source)
XLA Modules:
  0.0 421.6 jit_solution(4991609013196547999)
XLA Ops:
  0.0 0.8 constant_dynamic-slice_fusion
  0.8 0.1 copy.95
  0.8 0.1 eq.76
  0.9 0.8 copy.99
  1.7 0.1 fusion.201
  1.8 0.2 reduce_window_sum.11
  1.9 0.2 select_reduce_fusion.1
  2.1 0.1 reduce_sum.93
  2.2 0.1 copy.96
  2.3 0.8 bitcast_add_fusion
  3.1 0.1 copy.97
  3.1 0.1 fusion.200
  3.3 0.1 select_reduce_fusion
  3.4 0.1 copy.98
  3.6 0.1 copy.100
  3.7 0.9 conditional.8
  3.7 0.8 copy.181
  4.5 0.7 collective-permute-start
  5.2 0.0 collective-permute-done
  5.2 0.9 broadcast_select_fusion
  6.1 7.2 %conditional.9 = (bf16[16,2048]{1,0:T(8,128)(2,1)S(1)}) conditional(s32[]{:T(128)} %convert_element_type.216, bf16[16,2048]{1,0:T(8,128)(2,1)S(1)} %broadcast_select_fusion, (bf16[16,2048]{1,0:T(8,128)(2,1)S(1)}, f32[1,2048]{1,0:T(1,128)}, bf16[32,5,16]{2,1,0:T(8,128)(2,1)S(1)}, bf16[2048,1536]{1,0:T(8,128)(2,1)}, bf16[768,2048]{1,0:T(8,128)(2,1)}, ...), branch_computations={%region_7.8_spmd, %region_8.10_spmd} | conditional | flops 1585070080 | bytes 37379364 | solution.py:64
  13.2 0.7 collective-permute-start.1
  13.9 0.0 collective-permute-done.1
  14.0 0.7 collective-permute-start.2
  14.7 0.0 collective-permute-done.2
  14.7 10.1 %conditional.11 = (bf16[16,2048]{1,0:T(8,128)(2,1)S(1)}) conditional(s32[]{:T(128)} %convert_element_type.214, bf16[16,2048]{1,0:T(8,128)(2,1)S(1)} %broadcast_select_fusion.2, (bf16[16,2048]{1,0:T(8,128)(2,1)S(1)}, f32[1,2048]{1,0:T(1,128)}, bf16[32,5,16]{2,1,0:T(8,128)(2,1)S(1)}, bf16[2048,1536]{1,0:T(8,128)(2,1)}, bf16[768,2048]{1,0:T(8,128)(2,1)}, ...), branch_computations={%region_13.14_spmd, %region_14.16_spmd} | conditional | flops 1585070080 | bytes 37379364 | solution.py:64
  24.8 0.7 collective-permute-start.3
  25.5 0.0 collective-permute-done.3
  25.6 0.7 collective-permute-start.4
  26.3 0.0 collective-permute-done.4
  26.3 9.9 %conditional.13 = (bf16[16,2048]{1,0:T(8,128)(2,1)S(1)}) conditional(s32[]{:T(128)} %convert_element_type.212, bf16[16,2048]{1,0:T(8,128)(2,1)S(1)} %broadcast_select_fusion.4, (bf16[16,2048]{1,0:T(8,128)(2,1)S(1)}, f32[1,2048]{1,0:T(1,128)}, bf16[32,5,16]{2,1,0:T(8,128)(2,1)S(1)}, bf16[2048,1536]{1,0:T(8,128)(2,1)}, bf16[768,2048]{1,0:T(8,128)(2,1)}, ...), branch_computations={%region_19.20_spmd, %region_20.22_spmd} | conditional | flops 1585070080 | bytes 37379364 | solution.py:64
  36.2 0.7 collective-permute-start.5
  36.9 0.0 collective-permute-done.5
  37.0 1.3 collective-permute-start.6
  38.3 334.5 %collective-permute-done.6 = bf16[16,2048]{1,0:T(8,128)(2,1)S(1)} collective-permute-done((bf16[16,2048]{1,0:T(8,128)(2,1)S(1)}, bf16[16,2048]{1,0:T(8,128)(2,1)S(1)}, u32[]{:S(2)}, u32[]{:S(2)}) %collective-permute-start.6) | collective-permute-done | bytes 65568 | tf_op jit(solution)/shard_map/ppermute | solution.py:67
  372.8 0.0 copy-start
  372.9 47.4 %conditional.15 = (bf16[16,2048]{1,0:T(8,128)(2,1)S(1)}) conditional(s32[]{:T(128)} %convert_element_type.210, bf16[16,2048]{1,0:T(8,128)(2,1)S(1)} %broadcast_select_fusion.6, (bf16[16,2048]{1,0:T(8,128)(2,1)S(1)}, f32[1,2048]{1,0:T(1,128)}, bf16[32,5,16]{2,1,0:T(8,128)(2,1)S(1)}, bf16[2048,1536]{1,0:T(8,128)(2,1)}, bf16[768,2048]{1,0:T(8,128)(2,1)}, ...), branch_computations={%region_25.26_spmd, %region_26.28_spmd} | conditional | flops 1585070080 | bytes 37379364 | solution.py:64
  372.9 0.1 fusion.190
  373.0 1.1 fusion.182
  374.1 0.4 copy.91
  374.5 0.8 reshape.187
  375.2 18.3 %all_to_all.78 = bf16[32,80,128]{2,1,0:T(8,128)(2,1)S(1)} all-to-all(bf16[32,80,128]{2,1,0:T(8,128)(2,1)S(1)} %reshape.187), channel_id=1, replica_groups=mesh['pp'=8,'ep'=32] {'ep'}, dimensions={0} | all-to-all | bytes 1310720 | tf_op jit(solution)/shard_map/cond/branch_1_fun/all_to_all | solution.py:38
  393.5 0.7 reshape.188
  394.2 0.0 copy-start.9
  394.2 4.4 %fusion.175 = f32[32,5,1536]{2,0,1:T(8,128)S(1)} fusion(bf16[2048,1536]{1,0:T(8,128)(2,1)} %get-tuple-element.178, bf16[32,5,2048]{2,1,0:T(8,128)(2,1)S(1)} %reshape.188), kind=kOutput, calls=%fused_computation.189 | convolution fusion | flops 1006632960 | bytes 7929856 | tf_op jit(solution)/shard_map/cond/branch_1_fun/gcd,dh->gch/dot_general | solution.py:47
  398.6 0.0 copy-done.9
  398.6 0.7 fusion.179
  399.4 0.4 copy.93
  399.7 0.8 reshape.189
  400.5 18.0 %all_to_all.79 = bf16[32,80,128]{2,1,0:T(8,128)(2,1)S(1)} all-to-all(bf16[32,80,128]{2,1,0:T(8,128)(2,1)S(1)} %reshape.189), channel_id=1, replica_groups=mesh['pp'=8,'ep'=32] {'ep'}, dimensions={0} | all-to-all | bytes 1310720 | tf_op jit(solution)/shard_map/cond/branch_1_fun/all_to_all | solution.py:38
  418.5 0.7 reshape.190
  419.2 0.7 fusion.184
  420.3 0.0 copy-done
  420.3 0.7 select_bitcast_fusion
  (19 shorter events, 0.2 us)
Async XLA Ops:
  4.5 0.7 collective-permute-start
  13.2 0.7 collective-permute-start.1
  14.0 0.7 collective-permute-start.2
  24.8 0.7 collective-permute-start.3
  25.6 0.7 collective-permute-start.4
  36.2 0.7 collective-permute-start.5
  37.0 335.8 %collective-permute-start.6 = (bf16[16,2048]{1,0:T(8,128)(2,1)S(1)}, bf16[16,2048]{1,0:T(8,128)(2,1)S(1)}, u32[]{:S(2)}, u32[]{:S(2)}) collective-permute-start(bf16[16,2048]{1,0:T(8,128)(2,1)S(1)} %get-tuple-element.283), channel_id=1, source_target_pairs={{192,224},{193,225},{194,226},{195,227},{196,228},{197,229},{198,2... | collective-permute-start | bytes 196616 | tf_op jit(solution)/shard_map/ppermute | solution.py:67
  372.8 47.4 %copy-start = (bf16[16,2048]{1,0:T(8,128)(2,1)S(1)}, bf16[16,2048]{1,0:T(8,128)(2,1)}, u32[]{:S(2)}) copy-start(bf16[16,2048]{1,0:T(8,128)(2,1)} %param.22) | copy-start | bytes 196612
  394.2 4.4 %copy-start.9 = (bf16[768,2048]{1,0:T(8,128)(2,1)S(1)}, bf16[768,2048]{1,0:T(8,128)(2,1)}, u32[]{:S(2)}) copy-start(bf16[768,2048]{1,0:T(8,128)(2,1)} %get-tuple-element.179) | copy-start | bytes 9437188 | tf_op jit(solution)/shard_map/cond
